TPU v7x, 128 devices: a whole 4x4x4 slice. The times are simulated.
128 devices in a mesh: row: 64 (over y, z, x_lo, core), rep: 2 (over x_hi).
Axes of the slice: x: 4 (x_hi: 2, x_lo: 2; x = x_hi * 2 + x_lo), y: 4, z: 4, core: 2. Of those that a mesh axis runs over, the one named last changes fastest.
Arguments:
- out_grad: bfloat16 [65536, 256], P(('row', 'rep')), may hold values from -6 to 6
- relu_mask: int32 [65536, 256], P(('row', 'rep')), may hold values 0 or 1
- features: bfloat16 [65536, 256], P('row'), may hold values from -6 to 6
- weight: bfloat16 [256, 256], replicated, may hold values from -0.375 to 0.375
- tile_cols: int32 [512, 128], P('row', 'rep'), may hold values from 0 to 255, as said below
- tile_counts: int32 [512, 2], P('row', 'rep'), may hold values from 1 to 64
- tile_values: bfloat16 [512, 128, 128, 128], P('row', 'rep')
Outputs:
- grad_in: bfloat16 [65536, 256], P(('row', 'rep'))
- grad_weight: float32 [256, 256], replicated
Inputs may be any that keep to these rules, and one draw needn't show every extreme that they name: `tile_cols`: the 64 entries of one row tile and one index of rep are distinct column tiles.
All inputs are finite; a program needn't handle non-finite values. No bound on the sum of `relu_mask` on one device may be relied on, other than what follows from the above.
Results may differ from a plain program's by a relative error of at most 0.0049.
Values may be sent and summed in bfloat16 or wider, within the bound.
No kernel may reach another device: no remote copies, remote signals or barrier semaphores. Data moves between devices by JAX's collectives and lax.ppermute only.
A program may use at most 320 MiB of HBM per device.

v0:
```python
import math

import jax
import jax.numpy as jnp
from jax import lax
from jax.sharding import PartitionSpec as P


def shards(out_grad, relu_mask, features, weight, tile_cols, tile_counts, tile_values):
    own_rows, feature_width = out_grad.shape
    row_tiles, most_slots = tile_cols.shape
    tile_size = tile_values.shape[-1]
    block_tiles = own_rows // tile_size
    column_tiles = block_tiles * lax.axis_size("row")
    gated = out_grad * relu_mask.astype(jnp.bfloat16)
    active = jnp.arange(most_slots, dtype=jnp.int32)[None, :] < tile_counts
    gathered = lax.all_gather(gated, "row", axis=0, tiled=True)
    grad_tiles = gathered.reshape(column_tiles, tile_size, feature_width)
    picked = jnp.take(grad_tiles, tile_cols, axis=0)
    picked = jnp.where(active[:, :, None, None], picked, jnp.zeros((), jnp.bfloat16))
    partial_sum = jnp.einsum(
        "tsab,tsbf->taf", tile_values, picked, preferred_element_type=jnp.float32
    )
    partial_sum = partial_sum.reshape(row_tiles * tile_size, feature_width)
    node_count = own_rows * lax.axis_size("row") * lax.axis_size("rep")
    normalizer = 1.0 / math.sqrt(node_count)
    propagated = lax.psum_scatter(partial_sum, "rep", scatter_dimension=0, tiled=True)
    own_features = lax.dynamic_slice_in_dim(features, lax.axis_index("rep") * own_rows, own_rows, 0)
    weight_term = jnp.dot(
        own_features.astype(jnp.float32).T, propagated, precision=lax.Precision.HIGHEST
    )
    grad_weight = lax.psum(weight_term * normalizer, ("row", "rep"))
    grad_in = jnp.dot(
        propagated.astype(jnp.bfloat16), weight.T, preferred_element_type=jnp.float32
    ).astype(jnp.bfloat16)
    return (grad_in, grad_weight)


def solution(mesh):
    in_specs = (
        P(("row", "rep"), None),
        P(("row", "rep"), None),
        P("row", None),
        P(),
        P("row", "rep"),
        P("row", "rep"),
        P("row", "rep", None, None),
    )
    out_specs = (P(("row", "rep"), None), P())
    return jax.shard_map(shards, mesh=mesh, in_specs=in_specs, out_specs=out_specs, check_vma=False)
```

profile of v0, /device:TPU:1, one launch (start us, length us, event | category | flops | bytes accessed | tf_op | source)
XLA Modules:
  0.0 355.5 jit_solution(13420820885882194405)
XLA Ops:
  7.2 0.0 copy-start
  7.2 0.0 all-gather.2.cloned.1.call-start
  7.2 1.9 convert_multiply_fusion
  9.1 0.0 all-gather.2.cloned.1.call-update
  9.2 0.0 reduce-scatter.2.cloned.1.call-start
  9.2 0.7 compare_select_fusion
  9.9 0.1 reshape.41
  10.0 0.8 iota_compare_fusion
  10.8 125.0 %all-gather.2.cloned.1.call-done = bf16[32768,256]{1,0:T(8,128)(2,1)} async-done(((bf16[512,256]{1,0:T(8,128)(2,1)}), bf16[32768,256]{1,0:T(8,128)(2,1)}) %all-gather.2.cloned.1.call-update) | async-done | bytes 16777232 | tf_op jit(solution)/shard_map/all_gather | solution.py:17
  135.8 21.9 %gather_fusion = bf16[512,128,256]{2,1,0:T(8,128)(2,1)} fusion(bf16[256,128,256]{2,1,0:T(8,128)(2,1)} %bitcast.12, s32[1024]{0:T(1024)S(1)} %pad_clamp_fusion), kind=kCustom, calls=%fused_computation | custom fusion | bytes 67110912 | tf_op jit(solution)/shard_map/jit(_take)/gather | solution.py:19
  157.7 0.0 copy-start.1
  157.7 18.6 %fusion = f32[8,256,128,1]{1,2,3,0:T(8,128)} fusion(bf16[8,64,128,128]{3,2,1,0:T(8,128)(2,1)} %param.13, bf16[8,64,128,256]{3,2,1,0:T(8,128)(2,1)} %bitcast.13, pred[8,64]{1,0:T(8,128)(4,1)S(1)} %get-tuple-element.3, pred[8,64]{1,0:T(8,128)(4,1)S(1)} %get-tuple-element.2), kind=kOutput, calls=%fused_computation.1 | convolution fusion | flops 4328521728 | bytes 51381248 | tf_op jit(solution)/shard_map/tsab,tsbf->taf/dot_general | solution.py:21
  176.3 0.0 reduce-scatter.2.cloned.1.call-update
  176.3 0.0 all-reduce.2.cloned.1.call-start
  176.3 22.8 %reduce-scatter.2.cloned.1.call-done = f32[512,256]{1,0:T(8,128)} async-done(((f32[1024,256]{1,0:T(8,128)}), f32[512,256]{1,0:T(8,128)}) %reduce-scatter.2.cloned.1.call-update) | async-done | bytes 524304 | tf_op jit(solution)/shard_map/reduce_scatter | solution.py:27
  199.2 0.0 copy-done
  199.2 2.2 convolution_multiply_fusion
  201.4 0.0 all-reduce.2.cloned.1.call-update
  201.4 0.0 copy-done.1
  201.4 2.0 convolution_convert_fusion
  203.4 143.9 %all-reduce.2.cloned.1.call-done = f32[256,256]{1,0:T(8,128)} async-done(((f32[256,256]{1,0:T(8,128)}), f32[256,256]{1,0:T(8,128)}) %all-reduce.2.cloned.1.call-update) | async-done | bytes 262160 | tf_op jit(solution)/shard_map/psum | solution.py:32
  347.3 1.7 copy.11
  (1 shorter events, 0.0 us)
Async XLA Ops:
  7.2 192.0 %copy-start = (bf16[1024,256]{1,0:T(8,128)(2,1)S(1)}, bf16[1024,256]{1,0:T(8,128)(2,1)}, u32[]{:S(2)}) copy-start(bf16[1024,256]{1,0:T(8,128)(2,1)} %param.9) | copy-start | bytes 1572868
  7.2 128.6 %all-gather.2.cloned.1.call-start = ((), (), s32[]{:S(2)}) async-start(), calls=%async_computation.1 | async-start | bytes 17039360 | tf_op jit(solution)/shard_map/all_gather | solution.py:17
  9.2 190.0 %reduce-scatter.2.cloned.1.call-start = ((), (), s32[]{:S(2)}) async-start(), calls=%async_computation.2 | async-start | bytes 1572864 | tf_op jit(solution)/shard_map/reduce_scatter | solution.py:27
  157.7 43.7 %copy-start.1 = (bf16[256,256]{1,0:T(8,128)(2,1)S(1)}, bf16[256,256]{1,0:T(8,128)(2,1)}, u32[]{:S(2)}) copy-start(bf16[256,256]{1,0:T(8,128)(2,1)} %param.10) | copy-start | bytes 393220
  176.3 171.0 %all-reduce.2.cloned.1.call-start = ((), (), s32[]{:S(2)}) async-start(), calls=%async_computation.3 | async-start | bytes 524288 | tf_op jit(solution)/shard_map/psum | solution.py:32
Sparse Core Ops, SparseCore 0:
  10.3 125.4 all-gather.1
  176.4 22.6 reduce-scatter.1
  204.5 142.7 all-reduce.1
where the time goes:
time: 356 us; the launch traced here: 355 us
  waiting for transfers between devices  292 us (82%)
  local copies, waits for them, and re-layouts  23.7 us (7%)
  matrix products  22.8 us (6%)
  between operations  13.8 us (4%)
    psum x1, waiting for transfers between devices, shards(): grad_weight = lax.psum(weight_term * normalizer, ('row', 'rep'))  144 us
    all_gather x1, waiting for transfers between devices, shards(): gathered = lax.all_gather(gated, 'row', axis=0, tiled=True)  125 us
    reduce_scatter x1, waiting for transfers between devices, shards(): lax.psum_scatter(partial_sum, 'rep', scatter_dimension=0, tiled=True)  22.8 us
    gather x1, local copies, waits for them, and re-layouts, shards(): picked = jnp.take(grad_tiles, tile_cols, axis=0)  21.9 us
    dot_general x1, matrix products, shards(): jnp.einsum('tsab,tsbf->taf', tile_values, picked, preferred_element_type=...  18.6 us
  transfers between devices with their start and end apart: 3, of which 3 were waited for; matrix products, arithmetic and copies ran while one was open for 1% of the time, Pallas kernels for 0%

commit v1 on v0

--- a/solution.py
+++ b/solution.py
@@ -4,6 +4,39 @@
 import jax.numpy as jnp
 from jax import lax
 from jax.sharding import PartitionSpec as P
+
+AXES = ("row", "rep")
+STAGES = ((1,), (2,), (3, 4), (5, 6), (0,))
+
+
+def xor_pairs(count, mask):
+    return [(i, i ^ mask) for i in range(count)]
+
+
+def butterfly_sum(x):
+    count = lax.axis_size("row") * lax.axis_size("rep")
+    idx = lax.axis_index(AXES)
+    buf = x
+    for bits in STAGES:
+        m = 1 << len(bits)
+        pos = sum(((idx >> b) & 1) << i for i, b in enumerate(bits))
+        parts = buf.reshape(m, buf.shape[0] // m, *buf.shape[1:])
+        acc = jnp.take(parts, pos, axis=0)
+        for d in range(1, m):
+            mask = sum(((d >> i) & 1) << b for i, b in enumerate(bits))
+            acc = acc + lax.ppermute(jnp.take(parts, pos ^ d, axis=0), AXES, xor_pairs(count, mask))
+        buf = acc
+    for bits in reversed(STAGES):
+        m = 1 << len(bits)
+        pos = sum(((idx >> b) & 1) << i for i, b in enumerate(bits))
+        got = [buf]
+        for d in range(1, m):
+            mask = sum(((d >> i) & 1) << b for i, b in enumerate(bits))
+            got.append(lax.ppermute(buf, AXES, xor_pairs(count, mask)))
+        stacked = jnp.stack(got)
+        order = jnp.arange(m, dtype=jnp.int32) ^ pos
+        buf = jnp.take(stacked, order, axis=0).reshape(m * buf.shape[0], *buf.shape[1:])
+    return buf
 
 
 def shards(out_grad, relu_mask, features, weight, tile_cols, tile_counts, tile_values):
@@ -24,12 +57,14 @@
     partial_sum = partial_sum.reshape(row_tiles * tile_size, feature_width)
     node_count = own_rows * lax.axis_size("row") * lax.axis_size("rep")
     normalizer = 1.0 / math.sqrt(node_count)
-    propagated = lax.psum_scatter(partial_sum, "rep", scatter_dimension=0, tiled=True)
-    own_features = lax.dynamic_slice_in_dim(features, lax.axis_index("rep") * own_rows, own_rows, 0)
     weight_term = jnp.dot(
-        own_features.astype(jnp.float32).T, propagated, precision=lax.Precision.HIGHEST
+        features.astype(jnp.float32).T, partial_sum, precision=lax.Precision.HIGHEST
     )
-    grad_weight = lax.psum(weight_term * normalizer, ("row", "rep"))
+    grad_weight = butterfly_sum(weight_term * normalizer)
+    rep = lax.axis_index("rep")
+    halves = partial_sum.reshape(2, own_rows, feature_width)
+    other = lax.ppermute(jnp.take(halves, 1 - rep, axis=0), "rep", [(0, 1), (1, 0)])
+    propagated = jnp.take(halves, rep, axis=0) + other
     grad_in = jnp.dot(
         propagated.astype(jnp.bfloat16), weight.T, preferred_element_type=jnp.float32
     ).astype(jnp.bfloat16)

time: 356 us -> 238 us (0.67)
  waiting for transfers between devices: 292 us -> 143 us
  starting transfers between devices: 0.12 us -> 29.9 us
    psum x1 -> x0, waiting for transfers between devices: 144 us -> none  [shards(): grad_weight = lax.psum(weight_term * normalizer, ('row', 'rep'))]
    ppermute x0 -> x19, starting transfers between devices: none -> 29.9 us  [the longest x9 19 us: butterfly_sum(): got.append(lax.ppermute(buf, AXES, xor_pairs(count, mask)))]
    reduce_scatter x1 -> x0, waiting for transfers between devices: 22.8 us -> none  [shards(): lax.psum_scatter(partial_sum, 'rep', scatter_dimension=0, tiled=True)]
    ppermute x0 -> x19, waiting for transfers between devices: none -> 18.2 us  [the longest x9 9.23 us: butterfly_sum(): got.append(lax.ppermute(buf, AXES, xor_pairs(count, mask)))]
  transfers between devices with their start and end apart: 3 -> 20, of which waited for: 3 -> 16; matrix products, arithmetic and copies ran while one was open for 1% -> 3% of each run, Pallas kernels for 0% -> 0%
where the time goes in v1:
time: 238 us; the launch traced here: 237 us
  waiting for transfers between devices  143 us (60%)
  starting transfers between devices  29.9 us (13%)
  local copies, waits for them, and re-layouts  25.7 us (11%)
  matrix products  19.3 us (8%)
  between operations  14.3 us (6%)
  other arithmetic  5.1 us (2%)
    all_gather x1, waiting for transfers between devices, shards(): gathered = lax.all_gather(gated, 'row', axis=0, tiled=True)  125 us
    gather x1, local copies, waits for them, and re-layouts, shards(): picked = jnp.take(grad_tiles, tile_cols, axis=0)  21.9 us
    ppermute x9, starting transfers between devices, butterfly_sum(): got.append(lax.ppermute(buf, AXES, xor_pairs(count, mask)))  19 us
    dot_general x1, matrix products, shards(): jnp.einsum('tsab,tsbf->taf', tile_values, picked, preferred_element_type=...  17.5 us
    ppermute x9, starting transfers between devices, butterfly_sum(): lax.ppermute(jnp.take(parts, pos ^ d, axis=0), AXES, xor_pairs(count, mask))  10 us
    ppermute x9, waiting for transfers between devices, butterfly_sum(): got.append(lax.ppermute(buf, AXES, xor_pairs(count, mask)))  9.23 us
    ppermute x9, waiting for transfers between devices, butterfly_sum(): lax.ppermute(jnp.take(parts, pos ^ d, axis=0), AXES, xor_pairs(count, mask))  8.92 us
  transfers between devices with their start and end apart: 20, of which 16 were waited for; matrix products, arithmetic and copies ran while one was open for 3% of the time, Pallas kernels for 0%

profile of v1, /device:TPU:1, one launch (start us, length us, event | category | flops | bytes accessed | tf_op | source)
XLA Modules:
  0.0 237.3 jit_solution(13082038283055042374)
XLA Ops:
  7.2 1.9 convert_multiply_fusion
  9.2 0.7 compare_select_fusion
  10.1 0.8 iota_compare_fusion
  10.9 124.9 %all-gather.2.cloned.1.call-done = bf16[32768,256]{1,0:T(8,128)(2,1)} async-done(((bf16[512,256]{1,0:T(8,128)(2,1)}), bf16[32768,256]{1,0:T(8,128)(2,1)}) %all-gather.2.cloned.1.call-update) | async-done | bytes 16777232 | tf_op jit(solution)/shard_map/all_gather | solution.py:50
  135.8 21.9 %gather_fusion = bf16[512,128,256]{2,1,0:T(8,128)(2,1)} fusion(bf16[256,128,256]{2,1,0:T(8,128)(2,1)} %bitcast.99, s32[1024]{0:T(1024)S(1)} %pad_clamp_fusion.5), kind=kCustom, calls=%fused_computation | custom fusion | bytes 67110912 | tf_op jit(solution)/shard_map/jit(_take)/gather | solution.py:52
  157.7 17.5 %fusion = f32[8,256,128,1]{1,2,3,0:T(8,128)S(1)} fusion(bf16[8,64,128,128]{3,2,1,0:T(8,128)(2,1)} %param.25, bf16[8,64,128,256]{3,2,1,0:T(8,128)(2,1)} %bitcast.100, pred[8,64]{1,0:T(8,128)(4,1)S(1)} %get-tuple-element.83, pred[8,64]{1,0:T(8,128)(4,1)S(1)} %get-tuple-element.82), kind=kOutput, calls=%fused_computation.6 | convolution fusion | flops 4328521728 | bytes 51381248 | tf_op jit(solution)/shard_map/tsab,tsbf->taf/dot_general | solution.py:54
  175.2 0.8 convolution_multiply_fusion
  176.1 0.4 collective-permute-start.1
  176.5 1.0 collective-permute-done.1
  177.5 0.7 collective-permute-start.2
  178.2 2.5 %collective-permute-done.2 = f32[64,256]{1,0:T(8,128)S(1)} collective-permute-done((f32[64,256]{1,0:T(8,128)S(1)}, f32[64,256]{1,0:T(8,128)S(1)}, u32[]{:S(2)}, u32[]{:S(2)}) %collective-permute-start.2) | collective-permute-done | bytes 65568 | tf_op jit(solution)/shard_map/ppermute | solution.py:27
  180.8 1.3 collective-permute-start.5
  182.1 1.3 collective-permute-start.4
  183.4 0.7 collective-permute-start.3
  184.1 0.5 collective-permute-done.5
  184.7 1.5 collective-permute-done.4
  186.3 1.5 collective-permute-start.8
  187.8 1.2 collective-permute-start.7
  189.1 0.6 collective-permute-start.6
  189.7 0.4 collective-permute-done.8
  190.1 1.7 collective-permute-done.7
  191.9 2.3 collective-permute-start.9
  194.4 0.1 broadcast_in_dim.181
  194.8 1.1 collective-permute-done.9
  195.9 2.2 collective-permute-start.10
  198.1 0.8 collective-permute-start
  199.0 0.8 collective-permute-done.10
  199.8 0.6 gather_fusion.1
  200.5 1.2 collective-permute-start.13
  201.7 0.8 collective-permute-start.12
  202.6 1.2 collective-permute-start.11
  203.8 0.3 collective-permute-done.13
  204.2 1.5 collective-permute-done.12
  205.7 0.6 gather_fusion.2
  206.4 1.6 collective-permute-start.16
  208.0 0.7 collective-permute-start.15
  208.7 0.9 collective-permute-start.14
  209.7 0.8 collective-permute-done.16
  210.5 1.9 collective-permute-done.15
  212.4 0.6 gather_fusion.3
  213.0 0.1 collective-permute-start.17
  213.2 3.0 %collective-permute-done.17 = f32[64,256]{1,0:T(8,128)S(1)} collective-permute-done((f32[64,256]{1,0:T(8,128)S(1)}, f32[64,256]{1,0:T(8,128)S(1)}, u32[]{:S(2)}, u32[]{:S(2)}) %collective-permute-start.17) | collective-permute-done | bytes 65568 | tf_op jit(solution)/shard_map/ppermute | solution.py:35
  216.2 0.6 gather_fusion.4
  216.9 10.2 %collective-permute-start.18 = (f32[128,256]{1,0:T(8,128)S(1)}, f32[128,256]{1,0:T(8,128)S(1)}, u32[]{:S(2)}, u32[]{:S(2)}) collective-permute-start(f32[128,256]{1,0:T(8,128)S(1)} %bitcast_select_fusion.1), channel_id=1, source_target_pairs={{0,2},{1,3},{2,0},{3,1},{4,6},{5,7},{6,4},{7,5},{8,10},{9,11},{10,... | collective-permute-start | bytes 393224 | tf_op jit(solution)/shard_map/ppermute | solution.py:35
  227.1 0.9 collective-permute-done.18
  228.1 0.6 gather_fusion.5
  228.6 0.8 bitcast_select_fusion
  229.4 1.0 convolution_convert_fusion
  (65 shorter events, 1.9 us)
Async XLA Ops:
  7.2 168.1 %copy-start = (bf16[1024,256]{1,0:T(8,128)(2,1)S(1)}, bf16[1024,256]{1,0:T(8,128)(2,1)}, u32[]{:S(2)}) copy-start(bf16[1024,256]{1,0:T(8,128)(2,1)} %param.21) | copy-start | bytes 1572868
  7.2 128.6 %all-gather.2.cloned.1.call-start = ((), (), s32[]{:S(2)}) async-start(), calls=%async_computation | async-start | bytes 17039360 | tf_op jit(solution)/shard_map/all_gather | solution.py:50
  157.7 71.7 %copy-start.1 = (bf16[256,256]{1,0:T(8,128)(2,1)S(1)}, bf16[256,256]{1,0:T(8,128)(2,1)}, u32[]{:S(2)}) copy-start(bf16[256,256]{1,0:T(8,128)(2,1)} %param.22) | copy-start | bytes 393220
  176.1 1.4 collective-permute-start.1
  177.5 3.2 %collective-permute-start.2 = (f32[64,256]{1,0:T(8,128)S(1)}, f32[64,256]{1,0:T(8,128)S(1)}, u32[]{:S(2)}, u32[]{:S(2)}) collective-permute-start(f32[64,256]{1,0:T(8,128)S(1)} %select_bitcast_fusion.2), channel_id=1, source_target_pairs={{0,4},{1,5},{2,6},{3,7},{4,0},{5,1},{6,2},{7,3},{8,12},{9,13},{10,... | collective-permute-start | bytes 196616 | tf_op jit(solution)/shard_map/ppermute | solution.py:27
  180.8 3.9 %collective-permute-start.5 = (f32[16,256]{1,0:T(8,128)S(1)}, f32[16,256]{1,0:T(8,128)S(1)}, u32[]{:S(2)}, u32[]{:S(2)}) collective-permute-start(f32[16,256]{1,0:T(8,128)S(1)} %get-tuple-element.75), channel_id=1, source_target_pairs={{0,24},{1,25},{2,26},{3,27},{4,28},{5,29},{6,30},{7,31},{8,16},{9,... | collective-permute-start | bytes 49160 | tf_op jit(solution)/shard_map/ppermute | solution.py:27
  182.1 4.1 %collective-permute-start.4 = (f32[16,256]{1,0:T(8,128)S(1)}, f32[16,256]{1,0:T(8,128)S(1)}, u32[]{:S(2)}, u32[]{:S(2)}) collective-permute-start(f32[16,256]{1,0:T(8,128)S(1)} %get-tuple-element.76), channel_id=1, source_target_pairs={{0,16},{1,17},{2,18},{3,19},{4,20},{5,21},{6,22},{7,23},{8,24},{9,... | collective-permute-start | bytes 49160 | tf_op jit(solution)/shard_map/ppermute | solution.py:27
  183.4 2.9 %collective-permute-start.3 = (f32[16,256]{1,0:T(8,128)S(1)}, f32[16,256]{1,0:T(8,128)S(1)}, u32[]{:S(2)}, u32[]{:S(2)}) collective-permute-start(f32[16,256]{1,0:T(8,128)S(1)} %get-tuple-element.74), channel_id=1, source_target_pairs={{0,8},{1,9},{2,10},{3,11},{4,12},{5,13},{6,14},{7,15},{8,0},{9,1},... | collective-permute-start | bytes 49160 | tf_op jit(solution)/shard_map/ppermute | solution.py:27
  186.3 3.7 %collective-permute-start.8 = (f32[4,256]{1,0:T(4,128)S(1)}, f32[4,256]{1,0:T(4,128)S(1)}, u32[]{:S(2)}, u32[]{:S(2)}) collective-permute-start(f32[4,256]{1,0:T(4,128)S(1)} %get-tuple-element.78), channel_id=1, source_target_pairs={{0,96},{1,97},{2,98},{3,99},{4,100},{5,101},{6,102},{7,103},{8,104... | collective-permute-start | bytes 12296 | tf_op jit(solution)/shard_map/ppermute | solution.py:27
  187.8 4.0 %collective-permute-start.7 = (f32[4,256]{1,0:T(4,128)S(1)}, f32[4,256]{1,0:T(4,128)S(1)}, u32[]{:S(2)}, u32[]{:S(2)}) collective-permute-start(f32[4,256]{1,0:T(4,128)S(1)} %get-tuple-element.79), channel_id=1, source_target_pairs={{0,64},{1,65},{2,66},{3,67},{4,68},{5,69},{6,70},{7,71},{8,72},{9,... | collective-permute-start | bytes 12296 | tf_op jit(solution)/shard_map/ppermute | solution.py:27
  189.1 2.8 %collective-permute-start.6 = (f32[4,256]{1,0:T(4,128)S(1)}, f32[4,256]{1,0:T(4,128)S(1)}, u32[]{:S(2)}, u32[]{:S(2)}) collective-permute-start(f32[4,256]{1,0:T(4,128)S(1)} %get-tuple-element.77), channel_id=1, source_target_pairs={{0,32},{1,33},{2,34},{3,35},{4,36},{5,37},{6,38},{7,39},{8,40},{9,... | collective-permute-start | bytes 12296 | tf_op jit(solution)/shard_map/ppermute | solution.py:27
  191.9 4.0 %collective-permute-start.9 = (f32[2,256]{1,0:T(2,128)S(1)}, f32[2,256]{1,0:T(2,128)S(1)}, u32[]{:S(2)}, u32[]{:S(2)}) collective-permute-start(f32[2,256]{1,0:T(2,128)S(1)} %fusion.20), channel_id=1, source_target_pairs={{0,1},{1,0},{2,3},{3,2},{4,5},{5,4},{6,7},{7,6},{8,9},{9,8},{10,11... | collective-permute-start | bytes 6152 | tf_op jit(solution)/shard_map/ppermute | solution.py:27
  195.9 3.9 %collective-permute-start.10 = (f32[2,256]{1,0:T(2,128)S(1)}, f32[2,256]{1,0:T(2,128)S(1)}, u32[]{:S(2)}, u32[]{:S(2)}) collective-permute-start(f32[2,256]{1,0:T(2,128)S(1)} %fusion.18), channel_id=1, source_target_pairs={{0,1},{1,0},{2,3},{3,2},{4,5},{5,4},{6,7},{7,6},{8,9},{9,8},{10,11... | collective-permute-start | bytes 6152 | tf_op jit(solution)/shard_map/ppermute | solution.py:35
  198.1 31.3 %collective-permute-start = (f32[512,256]{1,0:T(8,128)S(1)}, f32[512,256]{1,0:T(8,128)S(1)}, u32[]{:S(2)}, u32[]{:S(2)}) collective-permute-start(f32[512,256]{1,0:T(8,128)S(1)} %select_bitcast_fusion), channel_id=1, source_target_pairs={{0,1},{1,0},{2,3},{3,2},{4,5},{5,4},{6,7},{7,6},{8,9},{9,8},{10,11... | collective-permute-start | bytes 1572872 | tf_op jit(solution)/shard_map/ppermute | solution.py:66
  200.5 3.7 %collective-permute-start.13 = (f32[4,256]{1,0:T(4,128)S(1)}, f32[4,256]{1,0:T(4,128)S(1)}, u32[]{:S(2)}, u32[]{:S(2)}) collective-permute-start(f32[4,256]{1,0:T(4,128)S(1)} %broadcast_select_fusion.3), channel_id=1, source_target_pairs={{0,96},{1,97},{2,98},{3,99},{4,100},{5,101},{6,102},{7,103},{8,104... | collective-permute-start | bytes 12296 | tf_op jit(solution)/shard_map/ppermute | solution.py:35
  201.7 4.0 %collective-permute-start.12 = (f32[4,256]{1,0:T(4,128)S(1)}, f32[4,256]{1,0:T(4,128)S(1)}, u32[]{:S(2)}, u32[]{:S(2)}) collective-permute-start(f32[4,256]{1,0:T(4,128)S(1)} %broadcast_select_fusion.3), channel_id=1, source_target_pairs={{0,64},{1,65},{2,66},{3,67},{4,68},{5,69},{6,70},{7,71},{8,72},{9,... | collective-permute-start | bytes 12296 | tf_op jit(solution)/shard_map/ppermute | solution.py:35
  202.6 3.1 %collective-permute-start.11 = (f32[4,256]{1,0:T(4,128)S(1)}, f32[4,256]{1,0:T(4,128)S(1)}, u32[]{:S(2)}, u32[]{:S(2)}) collective-permute-start(f32[4,256]{1,0:T(4,128)S(1)} %broadcast_select_fusion.3), channel_id=1, source_target_pairs={{0,32},{1,33},{2,34},{3,35},{4,36},{5,37},{6,38},{7,39},{8,40},{9,... | collective-permute-start | bytes 12296 | tf_op jit(solution)/shard_map/ppermute | solution.py:35
  206.4 4.1 %collective-permute-start.16 = (f32[16,256]{1,0:T(8,128)S(1)}, f32[16,256]{1,0:T(8,128)S(1)}, u32[]{:S(2)}, u32[]{:S(2)}) collective-permute-start(f32[16,256]{1,0:T(8,128)S(1)} %broadcast_select_fusion.1), channel_id=1, source_target_pairs={{0,24},{1,25},{2,26},{3,27},{4,28},{5,29},{6,30},{7,31},{8,16},{9,... | collective-permute-start | bytes 49160 | tf_op jit(solution)/shard_map/ppermute | solution.py:35
  208.0 4.4 %collective-permute-start.15 = (f32[16,256]{1,0:T(8,128)S(1)}, f32[16,256]{1,0:T(8,128)S(1)}, u32[]{:S(2)}, u32[]{:S(2)}) collective-permute-start(f32[16,256]{1,0:T(8,128)S(1)} %broadcast_select_fusion.1), channel_id=1, source_target_pairs={{0,16},{1,17},{2,18},{3,19},{4,20},{5,21},{6,22},{7,23},{8,24},{9,... | collective-permute-start | bytes 49160 | tf_op jit(solution)/shard_map/ppermute | solution.py:35
  208.7 3.7 %collective-permute-start.14 = (f32[16,256]{1,0:T(8,128)S(1)}, f32[16,256]{1,0:T(8,128)S(1)}, u32[]{:S(2)}, u32[]{:S(2)}) collective-permute-start(f32[16,256]{1,0:T(8,128)S(1)} %broadcast_select_fusion.1), channel_id=1, source_target_pairs={{0,8},{1,9},{2,10},{3,11},{4,12},{5,13},{6,14},{7,15},{8,0},{9,1},... | collective-permute-start | bytes 49160 | tf_op jit(solution)/shard_map/ppermute | solution.py:35
  213.0 3.2 %collective-permute-start.17 = (f32[64,256]{1,0:T(8,128)S(1)}, f32[64,256]{1,0:T(8,128)S(1)}, u32[]{:S(2)}, u32[]{:S(2)}) collective-permute-start(f32[64,256]{1,0:T(8,128)S(1)} %bitcast_select_fusion.3), channel_id=1, source_target_pairs={{0,4},{1,5},{2,6},{3,7},{4,0},{5,1},{6,2},{7,3},{8,12},{9,13},{10,... | collective-permute-start | bytes 196616 | tf_op jit(solution)/shard_map/ppermute | solution.py:35
  216.9 11.2 %collective-permute-start.18 = (f32[128,256]{1,0:T(8,128)S(1)}, f32[128,256]{1,0:T(8,128)S(1)}, u32[]{:S(2)}, u32[]{:S(2)}) collective-permute-start(f32[128,256]{1,0:T(8,128)S(1)} %bitcast_select_fusion.1), channel_id=1, source_target_pairs={{0,2},{1,3},{2,0},{3,1},{4,6},{5,7},{6,4},{7,5},{8,10},{9,11},{10,... | collective-permute-start | bytes 393224 | tf_op jit(solution)/shard_map/ppermute | solution.py:35
Sparse Core Ops, SparseCore 0:
  10.3 125.4 all-gather.1

commit v2 on v0

--- a/solution.py
+++ b/solution.py
@@ -4,6 +4,45 @@
 import jax.numpy as jnp
 from jax import lax
 from jax.sharding import PartitionSpec as P
+
+AXES = ("row", "rep")
+CORE_BIT = 1
+DOUBLING_STAGES = ((2, 0), (3, 4), (5, 6))
+
+
+def xor_pairs(count, mask):
+    return [(i, i ^ mask) for i in range(count)]
+
+
+def group_mask(d, bits):
+    return sum(((d >> i) & 1) << b for i, b in enumerate(bits))
+
+
+def group_pos(idx, bits):
+    return sum(((idx >> b) & 1) << i for i, b in enumerate(bits))
+
+
+def butterfly_sum(x):
+    count = lax.axis_size("row") * lax.axis_size("rep")
+    idx = lax.axis_index(AXES)
+    core = (idx >> CORE_BIT) & 1
+    core_mask = 1 << CORE_BIT
+    parts = x.reshape(2, x.shape[0] // 2, *x.shape[1:])
+    mine = jnp.take(parts, core, axis=0)
+    other = lax.ppermute(jnp.take(parts, 1 - core, axis=0), AXES, xor_pairs(count, core_mask))
+    buf = jnp.where(core == 0, mine + other, other + mine)
+    for bits in DOUBLING_STAGES:
+        m = 1 << len(bits)
+        pos = group_pos(idx, bits)
+        got = [buf] + [
+            lax.ppermute(buf, AXES, xor_pairs(count, group_mask(d, bits))) for d in range(1, m)
+        ]
+        ordered = jnp.take(jnp.stack(got), jnp.arange(m, dtype=jnp.int32) ^ pos, axis=0)
+        buf = ordered[0]
+        for j in range(1, m):
+            buf = buf + ordered[j]
+    got = lax.ppermute(buf, AXES, xor_pairs(count, core_mask))
+    return jnp.where(core == 0, jnp.concatenate([buf, got]), jnp.concatenate([got, buf]))
 
 
 def shards(out_grad, relu_mask, features, weight, tile_cols, tile_counts, tile_values):
@@ -24,12 +63,14 @@
     partial_sum = partial_sum.reshape(row_tiles * tile_size, feature_width)
     node_count = own_rows * lax.axis_size("row") * lax.axis_size("rep")
     normalizer = 1.0 / math.sqrt(node_count)
-    propagated = lax.psum_scatter(partial_sum, "rep", scatter_dimension=0, tiled=True)
-    own_features = lax.dynamic_slice_in_dim(features, lax.axis_index("rep") * own_rows, own_rows, 0)
     weight_term = jnp.dot(
-        own_features.astype(jnp.float32).T, propagated, precision=lax.Precision.HIGHEST
+        features.astype(jnp.float32).T, partial_sum, precision=lax.Precision.HIGHEST
     )
-    grad_weight = lax.psum(weight_term * normalizer, ("row", "rep"))
+    grad_weight = butterfly_sum(weight_term * normalizer)
+    rep = lax.axis_index("rep")
+    halves = partial_sum.reshape(2, own_rows, feature_width)
+    other = lax.ppermute(jnp.take(halves, 1 - rep, axis=0), "rep", [(0, 1), (1, 0)])
+    propagated = jnp.take(halves, rep, axis=0) + other
     grad_in = jnp.dot(
         propagated.astype(jnp.bfloat16), weight.T, preferred_element_type=jnp.float32
     ).astype(jnp.bfloat16)

time: 356 us -> 218 us (0.61)
  waiting for transfers between devices: 292 us -> 137 us
  starting transfers between devices: 0.12 us -> 17.6 us
    psum x1 -> x0, waiting for transfers between devices: 144 us -> none  [shards(): grad_weight = lax.psum(weight_term * normalizer, ('row', 'rep'))]
    reduce_scatter x1 -> x0, waiting for transfers between devices: 22.8 us -> none  [shards(): lax.psum_scatter(partial_sum, 'rep', scatter_dimension=0, tiled=True)]
    ppermute x0 -> x12, starting transfers between devices: none -> 17.6 us  [the longest x9 10 us: butterfly_sum(): lax.ppermute(buf, AXES, xor_pairs(count, group_mask(d, bits)))]
    ppermute x0 -> x12, waiting for transfers between devices: none -> 12.5 us  [the longest x9 11.4 us: butterfly_sum(): lax.ppermute(buf, AXES, xor_pairs(count, group_mask(d, bits)))]
  transfers between devices with their start and end apart: 3 -> 13, of which waited for: 3 -> 11; matrix products, arithmetic and copies ran while one was open for 1% -> 3% of each run, Pallas kernels for 0% -> 0%
where the time goes in v2:
time: 218 us
  waiting for transfers between devices  137 us (63%)
  local copies, waits for them, and re-layouts  23.8 us (11%)
  matrix products  20.3 us (9%)
  starting transfers between devices  17.6 us (8%)
  between operations  14.2 us (7%)
  other arithmetic  4.84 us (2%)
    all_gather x1, waiting for transfers between devices, shards(): gathered = lax.all_gather(gated, 'row', axis=0, tiled=True)  125 us
    gather x1, local copies, waits for them, and re-layouts, shards(): picked = jnp.take(grad_tiles, tile_cols, axis=0)  21.9 us
    dot_general x1, matrix products, shards(): jnp.einsum('tsab,tsbf->taf', tile_values, picked, preferred_element_type=...  17.5 us
    ppermute x9, waiting for transfers between devices, butterfly_sum(): lax.ppermute(buf, AXES, xor_pairs(count, group_mask(d, bits)))  11.4 us
    ppermute x9, starting transfers between devices, butterfly_sum(): lax.ppermute(buf, AXES, xor_pairs(count, group_mask(d, bits)))  10 us
    ppermute x1, starting transfers between devices, butterfly_sum(): got = lax.ppermute(buf, AXES, xor_pairs(count, core_mask))  4.91 us
  transfers between devices with their start and end apart: 13, of which 11 were waited for; matrix products, arithmetic and copies ran while one was open for 3% of the time, Pallas kernels for 0%

profile of v2, /device:TPU:1, one launch (start us, length us, event | category | flops | bytes accessed | tf_op | source)
XLA Modules:
  0.0 218.2 jit_solution(8378743402661240332)
XLA Ops:
  7.2 0.0 copy-start
  7.2 0.0 all-gather.2.cloned.1.call-start
  7.2 1.9 convert_multiply_fusion
  9.1 0.0 all-gather.2.cloned.1.call-update
  9.2 0.7 compare_select_fusion
  9.9 0.1 reshape.175
  10.0 0.8 iota_compare_fusion
  10.8 125.0 %all-gather.2.cloned.1.call-done = bf16[32768,256]{1,0:T(8,128)(2,1)} async-done(((bf16[512,256]{1,0:T(8,128)(2,1)}), bf16[32768,256]{1,0:T(8,128)(2,1)}) %all-gather.2.cloned.1.call-update) | async-done | bytes 16777232 | tf_op jit(solution)/shard_map/all_gather | solution.py:56
  135.8 21.9 %gather_fusion = bf16[512,128,256]{2,1,0:T(8,128)(2,1)} fusion(bf16[256,128,256]{2,1,0:T(8,128)(2,1)} %bitcast.45, s32[1024]{0:T(1024)S(1)} %pad_clamp_fusion.3), kind=kCustom, calls=%fused_computation.3 | custom fusion | bytes 67110912 | tf_op jit(solution)/shard_map/jit(_take)/gather | solution.py:58
  157.7 0.0 copy-start.1
  157.7 17.5 %fusion = f32[8,256,128,1]{1,2,3,0:T(8,128)S(1)} fusion(bf16[8,64,128,128]{3,2,1,0:T(8,128)(2,1)} %param.19, bf16[8,64,128,256]{3,2,1,0:T(8,128)(2,1)} %bitcast.46, pred[8,64]{1,0:T(8,128)(4,1)S(1)} %get-tuple-element.28, pred[8,64]{1,0:T(8,128)(4,1)S(1)} %get-tuple-element.27), kind=kOutput, calls=%fused_computation.4 | convolution fusion | flops 4328521728 | bytes 51381248 | tf_op jit(solution)/shard_map/tsab,tsbf->taf/dot_general | solution.py:60
  175.2 0.0 copy-done
  175.2 0.8 convolution_multiply_fusion
  176.1 0.4 collective-permute-start.1
  176.4 1.0 collective-permute-done.1
  177.5 1.9 collective-permute-start.4
  179.4 0.6 collective-permute-start.3
  180.0 0.8 collective-permute-start.2
  180.9 2.3 %collective-permute-start = (f32[512,256]{1,0:T(8,128)S(1)}, f32[512,256]{1,0:T(8,128)}, u32[]{:S(2)}, u32[]{:S(2)}) collective-permute-start(f32[512,256]{1,0:T(8,128)S(1)} %select_bitcast_fusion), channel_id=1, source_target_pairs={{0,1},{1,0},{2,3},{3,2},{4,5},{5,4},{6,7},{7,6},{8,9},{9,8},{10,11... | collective-permute-start | bytes 1572872 | tf_op jit(solution)/shard_map/ppermute | solution.py:72
  183.2 1.1 collective-permute-done.4
  184.2 1.3 collective-permute-done.3
  185.5 1.2 collective-permute-done.2
  186.8 0.6 gather_fusion.1
  187.4 0.1 broadcast_select_fusion.2
  187.5 1.4 collective-permute-start.7
  188.9 1.3 collective-permute-start.6
  190.2 0.7 collective-permute-start.5
  190.9 2.1 collective-permute-done.7
  193.1 1.6 collective-permute-done.6
  194.6 0.4 collective-permute-done.5
  195.1 0.6 gather_fusion.2
  195.7 0.1 broadcast_select_fusion.1
  195.8 1.5 collective-permute-start.10
  197.3 1.0 collective-permute-start.9
  198.3 0.9 collective-permute-start.8
  199.2 1.7 collective-permute-done.10
  200.9 1.7 collective-permute-done.9
  202.6 0.3 collective-permute-done.8
  203.0 0.6 gather_fusion.3
  203.5 0.1 broadcast_select_fusion
  203.7 4.9 %collective-permute-start.11 = (f32[128,256]{1,0:T(8,128)S(1)}, f32[128,256]{1,0:T(8,128)S(1)}, u32[]{:S(2)}, u32[]{:S(2)}) collective-permute-start(f32[128,256]{1,0:T(8,128)S(1)} %fusion.11), channel_id=1, source_target_pairs={{0,2},{1,3},{2,0},{3,1},{4,6},{5,7},{6,4},{7,5},{8,10},{9,11},{10,... | collective-permute-start | bytes 393224 | tf_op jit(solution)/shard_map/ppermute | solution.py:44
  208.6 0.0 collective-permute-done
  208.6 0.0 copy-done.1
  208.6 2.0 convolution_convert_fusion
  210.6 0.0 collective-permute-done.11
  210.6 0.7 maximum_select_fusion
  (20 shorter events, 0.4 us)
Async XLA Ops:
  7.2 168.1 %copy-start = (bf16[1024,256]{1,0:T(8,128)(2,1)S(1)}, bf16[1024,256]{1,0:T(8,128)(2,1)}, u32[]{:S(2)}) copy-start(bf16[1024,256]{1,0:T(8,128)(2,1)} %param.15) | copy-start | bytes 1572868
  7.2 128.6 %all-gather.2.cloned.1.call-start = ((), (), s32[]{:S(2)}) async-start(), calls=%async_computation | async-start | bytes 17039360 | tf_op jit(solution)/shard_map/all_gather | solution.py:56
  157.7 50.9 %copy-start.1 = (bf16[256,256]{1,0:T(8,128)(2,1)S(1)}, bf16[256,256]{1,0:T(8,128)(2,1)}, u32[]{:S(2)}) copy-start(bf16[256,256]{1,0:T(8,128)(2,1)} %param.16) | copy-start | bytes 393220
  176.1 1.4 collective-permute-start.1
  177.5 6.7 %collective-permute-start.4 = (f32[128,256]{1,0:T(8,128)S(1)}, f32[128,256]{1,0:T(8,128)S(1)}, u32[]{:S(2)}, u32[]{:S(2)}) collective-permute-start(f32[128,256]{1,0:T(8,128)S(1)} %bitcast_add_fusion.1), channel_id=1, source_target_pairs={{0,5},{1,4},{2,7},{3,6},{4,1},{5,0},{6,3},{7,2},{8,13},{9,12},{10,... | collective-permute-start | bytes 393224 | tf_op jit(solution)/shard_map/ppermute | solution.py:38
  179.4 6.1 %collective-permute-start.3 = (f32[128,256]{1,0:T(8,128)S(1)}, f32[128,256]{1,0:T(8,128)S(1)}, u32[]{:S(2)}, u32[]{:S(2)}) collective-permute-start(f32[128,256]{1,0:T(8,128)S(1)} %bitcast_add_fusion.1), channel_id=1, source_target_pairs={{0,1},{1,0},{2,3},{3,2},{4,5},{5,4},{6,7},{7,6},{8,9},{9,8},{10,11... | collective-permute-start | bytes 393224 | tf_op jit(solution)/shard_map/ppermute | solution.py:38
  180.0 6.7 %collective-permute-start.2 = (f32[128,256]{1,0:T(8,128)S(1)}, f32[128,256]{1,0:T(8,128)S(1)}, u32[]{:S(2)}, u32[]{:S(2)}) collective-permute-start(f32[128,256]{1,0:T(8,128)S(1)} %bitcast_add_fusion.1), channel_id=1, source_target_pairs={{0,4},{1,5},{2,6},{3,7},{4,0},{5,1},{6,2},{7,3},{8,12},{9,13},{10,... | collective-permute-start | bytes 393224 | tf_op jit(solution)/shard_map/ppermute | solution.py:38
  180.9 27.7 %collective-permute-start = (f32[512,256]{1,0:T(8,128)S(1)}, f32[512,256]{1,0:T(8,128)}, u32[]{:S(2)}, u32[]{:S(2)}) collective-permute-start(f32[512,256]{1,0:T(8,128)S(1)} %select_bitcast_fusion), channel_id=1, source_target_pairs={{0,1},{1,0},{2,3},{3,2},{4,5},{5,4},{6,7},{7,6},{8,9},{9,8},{10,11... | collective-permute-start | bytes 1572872 | tf_op jit(solution)/shard_map/ppermute | solution.py:72
  187.5 5.5 %collective-permute-start.7 = (f32[128,256]{1,0:T(8,128)S(1)}, f32[128,256]{1,0:T(8,128)S(1)}, u32[]{:S(2)}, u32[]{:S(2)}) collective-permute-start(f32[128,256]{1,0:T(8,128)S(1)} %fusion.21), channel_id=1, source_target_pairs={{0,24},{1,25},{2,26},{3,27},{4,28},{5,29},{6,30},{7,31},{8,16},{9,... | collective-permute-start | bytes 393224 | tf_op jit(solution)/shard_map/ppermute | solution.py:38
  188.9 5.7 %collective-permute-start.6 = (f32[128,256]{1,0:T(8,128)S(1)}, f32[128,256]{1,0:T(8,128)S(1)}, u32[]{:S(2)}, u32[]{:S(2)}) collective-permute-start(f32[128,256]{1,0:T(8,128)S(1)} %fusion.21), channel_id=1, source_target_pairs={{0,16},{1,17},{2,18},{3,19},{4,20},{5,21},{6,22},{7,23},{8,24},{9,... | collective-permute-start | bytes 393224 | tf_op jit(solution)/shard_map/ppermute | solution.py:38
  190.2 4.9 %collective-permute-start.5 = (f32[128,256]{1,0:T(8,128)S(1)}, f32[128,256]{1,0:T(8,128)S(1)}, u32[]{:S(2)}, u32[]{:S(2)}) collective-permute-start(f32[128,256]{1,0:T(8,128)S(1)} %fusion.21), channel_id=1, source_target_pairs={{0,8},{1,9},{2,10},{3,11},{4,12},{5,13},{6,14},{7,15},{8,0},{9,1},... | collective-permute-start | bytes 393224 | tf_op jit(solution)/shard_map/ppermute | solution.py:38
  195.8 5.1 %collective-permute-start.10 = (f32[128,256]{1,0:T(8,128)S(1)}, f32[128,256]{1,0:T(8,128)S(1)}, u32[]{:S(2)}, u32[]{:S(2)}) collective-permute-start(f32[128,256]{1,0:T(8,128)S(1)} %fusion.20), channel_id=1, source_target_pairs={{0,96},{1,97},{2,98},{3,99},{4,100},{5,101},{6,102},{7,103},{8,104... | collective-permute-start | bytes 393224 | tf_op jit(solution)/shard_map/ppermute | solution.py:38
  197.3 5.3 %collective-permute-start.9 = (f32[128,256]{1,0:T(8,128)S(1)}, f32[128,256]{1,0:T(8,128)S(1)}, u32[]{:S(2)}, u32[]{:S(2)}) collective-permute-start(f32[128,256]{1,0:T(8,128)S(1)} %fusion.20), channel_id=1, source_target_pairs={{0,64},{1,65},{2,66},{3,67},{4,68},{5,69},{6,70},{7,71},{8,72},{9,... | collective-permute-start | bytes 393224 | tf_op jit(solution)/shard_map/ppermute | solution.py:38
  198.3 4.7 %collective-permute-start.8 = (f32[128,256]{1,0:T(8,128)S(1)}, f32[128,256]{1,0:T(8,128)S(1)}, u32[]{:S(2)}, u32[]{:S(2)}) collective-permute-start(f32[128,256]{1,0:T(8,128)S(1)} %fusion.20), channel_id=1, source_target_pairs={{0,32},{1,33},{2,34},{3,35},{4,36},{5,37},{6,38},{7,39},{8,40},{9,... | collective-permute-start | bytes 393224 | tf_op jit(solution)/shard_map/ppermute | solution.py:38
  203.7 6.9 %collective-permute-start.11 = (f32[128,256]{1,0:T(8,128)S(1)}, f32[128,256]{1,0:T(8,128)S(1)}, u32[]{:S(2)}, u32[]{:S(2)}) collective-permute-start(f32[128,256]{1,0:T(8,128)S(1)} %fusion.11), channel_id=1, source_target_pairs={{0,2},{1,3},{2,0},{3,1},{4,6},{5,7},{6,4},{7,5},{8,10},{9,11},{10,... | collective-permute-start | bytes 393224 | tf_op jit(solution)/shard_map/ppermute | solution.py:44
Sparse Core Ops, SparseCore 0:
  10.3 125.4 all-gather.1

commit v3 on v2

--- a/solution.py
+++ b/solution.py
@@ -3,6 +3,8 @@
 import jax
 import jax.numpy as jnp
 from jax import lax
+from jax.experimental import pallas as pl
+from jax.experimental.pallas import tpu as pltpu
 from jax.sharding import PartitionSpec as P
 
 AXES = ("row", "rep")
@@ -45,6 +47,57 @@
     return jnp.where(core == 0, jnp.concatenate([buf, got]), jnp.concatenate([got, buf]))
 
 
+SLOT_GROUP = 16
+
+
+def tile_kernel(cols_ref, counts_ref, values_ref, grad_ref, out_ref):
+    t = pl.program_id(0)
+    count = counts_ref[t, 0]
+    slots = values_ref.shape[1]
+    out_ref[...] = jnp.zeros(out_ref.shape, out_ref.dtype)
+    for first in range(0, slots, SLOT_GROUP):
+
+        @pl.when(count > first)
+        def _():
+            acc = jnp.zeros(out_ref.shape[1:], jnp.float32)
+            for s in range(first, min(first + SLOT_GROUP, slots)):
+                live = jnp.where(s < count, 1.0, 0.0).astype(jnp.float32)
+                term = jnp.dot(
+                    values_ref[0, s], grad_ref[cols_ref[t, s]], preferred_element_type=jnp.float32
+                )
+                acc = acc + term * live
+            out_ref[0] += acc
+
+
+def propagate_tiles(tile_cols, tile_counts, tile_values, grad_tiles):
+    row_tiles, slots, tile_size, _ = tile_values.shape
+    column_tiles, _, width = grad_tiles.shape
+    grid_spec = pltpu.PrefetchScalarGridSpec(
+        num_scalar_prefetch=2,
+        grid=(row_tiles,),
+        in_specs=[
+            pl.BlockSpec((1, slots, tile_size, tile_size), lambda t, c, n: (t, 0, 0, 0)),
+            pl.BlockSpec(
+                (column_tiles, tile_size, width),
+                lambda t, c, n: (0, 0, 0),
+                pipeline_mode=pl.Buffered(1),
+            ),
+        ],
+        out_specs=pl.BlockSpec((1, tile_size, width), lambda t, c, n: (t, 0, 0)),
+    )
+    flops = 2 * row_tiles * slots * tile_size * tile_size * width
+    moved = tile_values.size * 2 + grad_tiles.size * 2 + row_tiles * tile_size * width * 4
+    return pl.pallas_call(
+        tile_kernel,
+        out_shape=jax.ShapeDtypeStruct((row_tiles, tile_size, width), jnp.float32),
+        grid_spec=grid_spec,
+        compiler_params=pltpu.CompilerParams(
+            dimension_semantics=("arbitrary",), vmem_limit_bytes=48 * 1024 * 1024
+        ),
+        cost_estimate=pl.CostEstimate(flops=flops, transcendentals=0, bytes_accessed=moved),
+    )(tile_cols, tile_counts, tile_values, grad_tiles)
+
+
 def shards(out_grad, relu_mask, features, weight, tile_cols, tile_counts, tile_values):
     own_rows, feature_width = out_grad.shape
     row_tiles, most_slots = tile_cols.shape
@@ -52,14 +105,9 @@
     block_tiles = own_rows // tile_size
     column_tiles = block_tiles * lax.axis_size("row")
     gated = out_grad * relu_mask.astype(jnp.bfloat16)
-    active = jnp.arange(most_slots, dtype=jnp.int32)[None, :] < tile_counts
     gathered = lax.all_gather(gated, "row", axis=0, tiled=True)
     grad_tiles = gathered.reshape(column_tiles, tile_size, feature_width)
-    picked = jnp.take(grad_tiles, tile_cols, axis=0)
-    picked = jnp.where(active[:, :, None, None], picked, jnp.zeros((), jnp.bfloat16))
-    partial_sum = jnp.einsum(
-        "tsab,tsbf->taf", tile_values, picked, preferred_element_type=jnp.float32
-    )
+    partial_sum = propagate_tiles(tile_cols, tile_counts, tile_values, grad_tiles)
     partial_sum = partial_sum.reshape(row_tiles * tile_size, feature_width)
     node_count = own_rows * lax.axis_size("row") * lax.axis_size("rep")
     normalizer = 1.0 / math.sqrt(node_count)

time: 218 us -> 200 us (0.917)
  local copies, waits for them, and re-layouts: 23.8 us -> 3.18 us
  matrix products: 20.3 us -> 2.81 us
  Pallas kernels: 0 us -> 16.7 us
  starting transfers between devices: 17.6 us -> 20.8 us
    gather x1 -> x0, local copies, waits for them, and re-layouts: 21.9 us -> none  [shards(): picked = jnp.take(grad_tiles, tile_cols, axis=0)]
    dot_general x1 -> x0, matrix products: 17.5 us -> none  [shards(): jnp.einsum('tsab,tsbf->taf', tile_values, picked, preferred_element_type=...]
    pallas_call x0 -> x1, Pallas kernels: none -> 16.7 us  [propagate_tiles(): pl.pallas_call(tile_kernel, out_shape=jax.ShapeDtypeStruct((row_tiles, ti...]
    ppermute x1, starting transfers between devices: 0.37 us -> 3.45 us  [butterfly_sum(): lax.ppermute(jnp.take(parts, 1 - core, axis=0), AXES, xor_pairs(count, co...]
  transfers between devices with their start and end apart: 13 -> 13, of which waited for: 11 -> 9; matrix products, arithmetic and copies ran while one was open for 3% -> 3% of each run, Pallas kernels for 0% -> 0%
where the time goes in v3:
time: 200 us; the launch traced here: 199 us
  waiting for transfers between devices  138 us (69%)
  starting transfers between devices  20.8 us (10%)
  Pallas kernels  16.7 us (8%)
  between operations  14.2 us (7%)
  other arithmetic  3.38 us (2%)
  local copies, waits for them, and re-layouts  3.18 us (2%)
  matrix products  2.81 us (1%)
    all_gather x1, waiting for transfers between devices, shards(): gathered = lax.all_gather(gated, 'row', axis=0, tiled=True)  126 us
    pallas_call x1, Pallas kernels, propagate_tiles(): pl.pallas_call(tile_kernel, out_shape=jax.ShapeDtypeStruct((row_tiles, ti...  16.7 us
    ppermute x9, waiting for transfers between devices, butterfly_sum(): lax.ppermute(buf, AXES, xor_pairs(count, group_mask(d, bits)))  11.4 us
    ppermute x9, starting transfers between devices, butterfly_sum(): lax.ppermute(buf, AXES, xor_pairs(count, group_mask(d, bits)))  10.2 us
    ppermute x1, starting transfers between devices, butterfly_sum(): got = lax.ppermute(buf, AXES, xor_pairs(count, core_mask))  4.66 us
  transfers between devices with their start and end apart: 13, of which 9 were waited for; matrix products, arithmetic and copies ran while one was open for 3% of the time, Pallas kernels for 0%

profile of v3, /device:TPU:1, one launch (start us, length us, event | category | flops | bytes accessed | tf_op | source)
XLA Modules:
  0.0 199.3 jit_solution(11495699854801359875)
XLA Ops:
  7.2 0.0 copy-start
  7.2 0.0 all-gather.2.cloned.1.call-start
  7.2 1.9 convert_multiply_fusion
  9.2 0.0 all-gather.2.cloned.1.call-update
  9.2 0.7 copy.9.counts_ref
  10.0 125.8 %all-gather.2.cloned.1.call-done = bf16[32768,256]{1,0:T(8,128)(2,1)} async-done(((bf16[512,256]{1,0:T(8,128)(2,1)}), bf16[32768,256]{1,0:T(8,128)(2,1)}) %all-gather.2.cloned.1.call-update) | async-done | bytes 16777232 | tf_op jit(solution)/shard_map/all_gather | solution.py:108
  135.8 0.0 copy-start.1
  135.8 0.7 copy-done.1
  136.5 0.0 copy-start.2
  136.5 16.7 %shard_map.86 = f32[8,128,256]{2,1,0:T(8,128)S(1)} custom-call(s32[8,64]{1,0:T(8,128)S(1)} %copy-done.1, s32[8,1]{1,0:T(8,128)S(1)} %copy.9.counts_ref, bf16[8,64,128,128]{3,2,1,0:T(8,128)(2,1)} %values_ref.1, bf16[256,128,256]{2,1,0:T(8,128)(2,1)} %bitcast.39), custom_call_target="tpu_custom_call" | custom-call | flops 4294967296 | bytes 34603008 | tf_op jit(solution)/shard_map/pallas_call | solution.py:90
  153.2 0.0 copy-done
  153.2 0.8 convolution_multiply_fusion
  154.0 3.4 %collective-permute-start.1 = (f32[128,256]{1,0:T(8,128)S(1)}, f32[128,256]{1,0:T(8,128)S(1)}, u32[]{:S(2)}, u32[]{:S(2)}) collective-permute-start(f32[128,256]{1,0:T(8,128)S(1)} %select_bitcast_fusion.1), channel_id=1, source_target_pairs={{0,2},{1,3},{2,0},{3,1},{4,6},{5,7},{6,4},{7,5},{8,10},{9,11},{10,... | collective-permute-start | bytes 393224 | tf_op jit(solution)/shard_map/ppermute | solution.py:34
  157.5 1.0 collective-permute-done.1
  158.4 2.9 %collective-permute-start.4 = (f32[128,256]{1,0:T(8,128)S(1)}, f32[128,256]{1,0:T(8,128)S(1)}, u32[]{:S(2)}, u32[]{:S(2)}) collective-permute-start(f32[128,256]{1,0:T(8,128)S(1)} %bitcast_add_fusion.1), channel_id=1, source_target_pairs={{0,5},{1,4},{2,7},{3,6},{4,1},{5,0},{6,3},{7,2},{8,13},{9,12},{10,... | collective-permute-start | bytes 393224 | tf_op jit(solution)/shard_map/ppermute | solution.py:40
  161.4 0.0 collective-permute-start.3
  161.4 0.7 collective-permute-start.2
  162.1 2.4 %collective-permute-start = (f32[512,256]{1,0:T(8,128)S(1)}, f32[512,256]{1,0:T(8,128)}, u32[]{:S(2)}, u32[]{:S(2)}) collective-permute-start(f32[512,256]{1,0:T(8,128)S(1)} %select_bitcast_fusion), channel_id=1, source_target_pairs={{0,1},{1,0},{2,3},{3,2},{4,5},{5,4},{6,7},{7,6},{8,9},{9,8},{10,11... | collective-permute-start | bytes 1572872 | tf_op jit(solution)/shard_map/ppermute | solution.py:120
  164.5 2.4 %collective-permute-done.4 = f32[128,256]{1,0:T(8,128)S(1)} collective-permute-done((f32[128,256]{1,0:T(8,128)S(1)}, f32[128,256]{1,0:T(8,128)S(1)}, u32[]{:S(2)}, u32[]{:S(2)}) %collective-permute-start.4) | collective-permute-done | bytes 131104 | tf_op jit(solution)/shard_map/ppermute | solution.py:40
  166.8 0.4 collective-permute-done.3
  167.3 0.8 collective-permute-done.2
  168.1 0.6 gather_fusion
  168.7 0.1 broadcast_select_fusion.2
  168.9 1.0 collective-permute-start.7
  169.9 1.2 collective-permute-start.6
  171.1 1.1 collective-permute-start.5
  172.2 3.6 %collective-permute-done.7 = f32[128,256]{1,0:T(8,128)S(1)} collective-permute-done((f32[128,256]{1,0:T(8,128)S(1)}, f32[128,256]{1,0:T(8,128)S(1)}, u32[]{:S(2)}, u32[]{:S(2)}) %collective-permute-start.7) | collective-permute-done | bytes 131104 | tf_op jit(solution)/shard_map/ppermute | solution.py:40
  175.8 0.0 collective-permute-done.6
  175.8 0.5 collective-permute-done.5
  176.4 0.6 gather_fusion.1
  177.0 0.1 broadcast_select_fusion.1
  177.1 0.5 collective-permute-start.10
  177.6 1.8 collective-permute-start.9
  179.4 1.0 collective-permute-start.8
  180.5 3.1 %collective-permute-done.10 = f32[128,256]{1,0:T(8,128)S(1)} collective-permute-done((f32[128,256]{1,0:T(8,128)S(1)}, f32[128,256]{1,0:T(8,128)S(1)}, u32[]{:S(2)}, u32[]{:S(2)}) %collective-permute-start.10) | collective-permute-done | bytes 131104 | tf_op jit(solution)/shard_map/ppermute | solution.py:40
  183.6 0.0 collective-permute-done.9
  183.6 0.6 collective-permute-done.8
  184.3 0.6 gather_fusion.2
  184.9 0.1 broadcast_select_fusion
  185.0 4.7 %collective-permute-start.11 = (f32[128,256]{1,0:T(8,128)S(1)}, f32[128,256]{1,0:T(8,128)S(1)}, u32[]{:S(2)}, u32[]{:S(2)}) collective-permute-start(f32[128,256]{1,0:T(8,128)S(1)} %fusion.4), channel_id=1, source_target_pairs={{0,2},{1,3},{2,0},{3,1},{4,6},{5,7},{6,4},{7,5},{8,10},{9,11},{10,... | collective-permute-start | bytes 393224 | tf_op jit(solution)/shard_map/ppermute | solution.py:46
  189.7 0.0 collective-permute-done
  189.7 0.0 copy-done.2
  189.7 2.0 %convolution_convert_fusion = bf16[512,256]{1,0:T(8,128)(2,1)} fusion(bf16[256,256]{1,0:T(8,128)(2,1)S(1)} %copy-done.2, f32[512,256]{1,0:T(8,128)} %collective-permute-done, f32[2,512,256]{2,1,0:T(8,128)S(1)} %bitcast.38, s32[]{:T(128)S(6)} %select_n.46, pred[]{:T(512)S(6)} %and.48), kind=kOutput, calls=%fused_computation.3 | convolution fusion | flops 67633152 | bytes 1441797 | tf_op jit(solution)/shard_map/dot_general | solution.py:122
  191.7 0.0 collective-permute-done.11
  191.7 0.7 maximum_select_fusion
  (19 shorter events, 0.4 us)
Async XLA Ops:
  7.2 146.0 %copy-start = (bf16[1024,256]{1,0:T(8,128)(2,1)S(1)}, bf16[1024,256]{1,0:T(8,128)(2,1)}, u32[]{:S(2)}) copy-start(bf16[1024,256]{1,0:T(8,128)(2,1)} %param.15) | copy-start | bytes 1572868
  7.2 128.6 %all-gather.2.cloned.1.call-start = ((), (), s32[]{:S(2)}) async-start(), calls=%async_computation | async-start | bytes 17039360 | tf_op jit(solution)/shard_map/all_gather | solution.py:108
  135.8 0.7 copy-start.1
  136.5 53.2 %copy-start.2 = (bf16[256,256]{1,0:T(8,128)(2,1)S(1)}, bf16[256,256]{1,0:T(8,128)(2,1)}, u32[]{:S(2)}) copy-start(bf16[256,256]{1,0:T(8,128)(2,1)} %param.16) | copy-start | bytes 393220
  154.0 4.4 %collective-permute-start.1 = (f32[128,256]{1,0:T(8,128)S(1)}, f32[128,256]{1,0:T(8,128)S(1)}, u32[]{:S(2)}, u32[]{:S(2)}) collective-permute-start(f32[128,256]{1,0:T(8,128)S(1)} %select_bitcast_fusion.1), channel_id=1, source_target_pairs={{0,2},{1,3},{2,0},{3,1},{4,6},{5,7},{6,4},{7,5},{8,10},{9,11},{10,... | collective-permute-start | bytes 393224 | tf_op jit(solution)/shard_map/ppermute | solution.py:34
  158.4 8.4 %collective-permute-start.4 = (f32[128,256]{1,0:T(8,128)S(1)}, f32[128,256]{1,0:T(8,128)S(1)}, u32[]{:S(2)}, u32[]{:S(2)}) collective-permute-start(f32[128,256]{1,0:T(8,128)S(1)} %bitcast_add_fusion.1), channel_id=1, source_target_pairs={{0,5},{1,4},{2,7},{3,6},{4,1},{5,0},{6,3},{7,2},{8,13},{9,12},{10,... | collective-permute-start | bytes 393224 | tf_op jit(solution)/shard_map/ppermute | solution.py:40
  161.4 5.9 %collective-permute-start.3 = (f32[128,256]{1,0:T(8,128)S(1)}, f32[128,256]{1,0:T(8,128)S(1)}, u32[]{:S(2)}, u32[]{:S(2)}) collective-permute-start(f32[128,256]{1,0:T(8,128)S(1)} %bitcast_add_fusion.1), channel_id=1, source_target_pairs={{0,1},{1,0},{2,3},{3,2},{4,5},{5,4},{6,7},{7,6},{8,9},{9,8},{10,11... | collective-permute-start | bytes 393224 | tf_op jit(solution)/shard_map/ppermute | solution.py:40
  161.4 6.7 %collective-permute-start.2 = (f32[128,256]{1,0:T(8,128)S(1)}, f32[128,256]{1,0:T(8,128)S(1)}, u32[]{:S(2)}, u32[]{:S(2)}) collective-permute-start(f32[128,256]{1,0:T(8,128)S(1)} %bitcast_add_fusion.1), channel_id=1, source_target_pairs={{0,4},{1,5},{2,6},{3,7},{4,0},{5,1},{6,2},{7,3},{8,12},{9,13},{10,... | collective-permute-start | bytes 393224 | tf_op jit(solution)/shard_map/ppermute | solution.py:40
  162.1 27.6 %collective-permute-start = (f32[512,256]{1,0:T(8,128)S(1)}, f32[512,256]{1,0:T(8,128)}, u32[]{:S(2)}, u32[]{:S(2)}) collective-permute-start(f32[512,256]{1,0:T(8,128)S(1)} %select_bitcast_fusion), channel_id=1, source_target_pairs={{0,1},{1,0},{2,3},{3,2},{4,5},{5,4},{6,7},{7,6},{8,9},{9,8},{10,11... | collective-permute-start | bytes 1572872 | tf_op jit(solution)/shard_map/ppermute | solution.py:120
  168.9 7.0 %collective-permute-start.7 = (f32[128,256]{1,0:T(8,128)S(1)}, f32[128,256]{1,0:T(8,128)S(1)}, u32[]{:S(2)}, u32[]{:S(2)}) collective-permute-start(f32[128,256]{1,0:T(8,128)S(1)} %fusion.11), channel_id=1, source_target_pairs={{0,24},{1,25},{2,26},{3,27},{4,28},{5,29},{6,30},{7,31},{8,16},{9,... | collective-permute-start | bytes 393224 | tf_op jit(solution)/shard_map/ppermute | solution.py:40
  169.9 5.9 %collective-permute-start.6 = (f32[128,256]{1,0:T(8,128)S(1)}, f32[128,256]{1,0:T(8,128)S(1)}, u32[]{:S(2)}, u32[]{:S(2)}) collective-permute-start(f32[128,256]{1,0:T(8,128)S(1)} %fusion.11), channel_id=1, source_target_pairs={{0,16},{1,17},{2,18},{3,19},{4,20},{5,21},{6,22},{7,23},{8,24},{9,... | collective-permute-start | bytes 393224 | tf_op jit(solution)/shard_map/ppermute | solution.py:40
  171.1 5.2 %collective-permute-start.5 = (f32[128,256]{1,0:T(8,128)S(1)}, f32[128,256]{1,0:T(8,128)S(1)}, u32[]{:S(2)}, u32[]{:S(2)}) collective-permute-start(f32[128,256]{1,0:T(8,128)S(1)} %fusion.11), channel_id=1, source_target_pairs={{0,8},{1,9},{2,10},{3,11},{4,12},{5,13},{6,14},{7,15},{8,0},{9,1},... | collective-permute-start | bytes 393224 | tf_op jit(solution)/shard_map/ppermute | solution.py:40
  177.1 6.5 %collective-permute-start.10 = (f32[128,256]{1,0:T(8,128)S(1)}, f32[128,256]{1,0:T(8,128)S(1)}, u32[]{:S(2)}, u32[]{:S(2)}) collective-permute-start(f32[128,256]{1,0:T(8,128)S(1)} %fusion.10), channel_id=1, source_target_pairs={{0,96},{1,97},{2,98},{3,99},{4,100},{5,101},{6,102},{7,103},{8,104... | collective-permute-start | bytes 393224 | tf_op jit(solution)/shard_map/ppermute | solution.py:40
  177.6 6.0 %collective-permute-start.9 = (f32[128,256]{1,0:T(8,128)S(1)}, f32[128,256]{1,0:T(8,128)S(1)}, u32[]{:S(2)}, u32[]{:S(2)}) collective-permute-start(f32[128,256]{1,0:T(8,128)S(1)} %fusion.10), channel_id=1, source_target_pairs={{0,64},{1,65},{2,66},{3,67},{4,68},{5,69},{6,70},{7,71},{8,72},{9,... | collective-permute-start | bytes 393224 | tf_op jit(solution)/shard_map/ppermute | solution.py:40
  179.4 4.8 %collective-permute-start.8 = (f32[128,256]{1,0:T(8,128)S(1)}, f32[128,256]{1,0:T(8,128)S(1)}, u32[]{:S(2)}, u32[]{:S(2)}) collective-permute-start(f32[128,256]{1,0:T(8,128)S(1)} %fusion.10), channel_id=1, source_target_pairs={{0,32},{1,33},{2,34},{3,35},{4,36},{5,37},{6,38},{7,39},{8,40},{9,... | collective-permute-start | bytes 393224 | tf_op jit(solution)/shard_map/ppermute | solution.py:40
  185.0 6.7 %collective-permute-start.11 = (f32[128,256]{1,0:T(8,128)S(1)}, f32[128,256]{1,0:T(8,128)S(1)}, u32[]{:S(2)}, u32[]{:S(2)}) collective-permute-start(f32[128,256]{1,0:T(8,128)S(1)} %fusion.4), channel_id=1, source_target_pairs={{0,2},{1,3},{2,0},{3,1},{4,6},{5,7},{6,4},{7,5},{8,10},{9,11},{10,... | collective-permute-start | bytes 393224 | tf_op jit(solution)/shard_map/ppermute | solution.py:46
Sparse Core Ops, SparseCore 0:
  10.3 125.4 all-gather.1

commit v4 on v3

--- a/solution.py
+++ b/solution.py
@@ -47,7 +47,7 @@
     return jnp.where(core == 0, jnp.concatenate([buf, got]), jnp.concatenate([got, buf]))
 
 
-SLOT_GROUP = 16
+SLOT_GROUP = 8
 
 
 def tile_kernel(cols_ref, counts_ref, values_ref, grad_ref, out_ref):

time: 200 us -> 203 us (1.015)
  Pallas kernels: 16.7 us -> 22.6 us
  starting transfers between devices: 20.8 us -> 16.8 us
    pallas_call x1, Pallas kernels: 16.7 us -> 22.6 us  [propagate_tiles(): pl.pallas_call(tile_kernel, out_shape=jax.ShapeDtypeStruct((row_tiles, ti...]
    ppermute x1, starting transfers between devices: 3.45 us -> 0.09 us  [butterfly_sum(): lax.ppermute(jnp.take(parts, 1 - core, axis=0), AXES, xor_pairs(count, co...]
where the time goes in v4:
time: 203 us
  waiting for transfers between devices  140 us (69%)
  Pallas kernels  22.6 us (11%)
  starting transfers between devices  16.8 us (8%)
  between operations  14.2 us (7%)
  other arithmetic  3.38 us (2%)
  local copies, waits for them, and re-layouts  3.18 us (2%)
  matrix products  2.81 us (1%)
    all_gather x1, waiting for transfers between devices, shards(): gathered = lax.all_gather(gated, 'row', axis=0, tiled=True)  126 us
    pallas_call x1, Pallas kernels, propagate_tiles(): pl.pallas_call(tile_kernel, out_shape=jax.ShapeDtypeStruct((row_tiles, ti...  22.6 us
    ppermute x9, waiting for transfers between devices, butterfly_sum(): lax.ppermute(buf, AXES, xor_pairs(count, group_mask(d, bits)))  12.8 us
    ppermute x9, starting transfers between devices, butterfly_sum(): lax.ppermute(buf, AXES, xor_pairs(count, group_mask(d, bits)))  10.3 us
    ppermute x1, starting transfers between devices, butterfly_sum(): got = lax.ppermute(buf, AXES, xor_pairs(count, core_mask))  5.08 us
  transfers between devices with their start and end apart: 13, of which 9 were waited for; matrix products, arithmetic and copies ran while one was open for 3% of the time, Pallas kernels for 0%

profile of v4, /device:TPU:1, one launch (start us, length us, event | category | flops | bytes accessed | tf_op | source)
XLA Modules:
  0.0 203.0 jit_solution(1300274691793513425)
XLA Ops:
  7.2 0.0 copy-start
  7.2 0.0 all-gather.2.cloned.1.call-start
  7.2 1.9 convert_multiply_fusion
  9.2 0.0 all-gather.2.cloned.1.call-update
  9.2 0.7 copy.9.counts_ref
  10.0 125.8 %all-gather.2.cloned.1.call-done = bf16[32768,256]{1,0:T(8,128)(2,1)} async-done(((bf16[512,256]{1,0:T(8,128)(2,1)}), bf16[32768,256]{1,0:T(8,128)(2,1)}) %all-gather.2.cloned.1.call-update) | async-done | bytes 16777232 | tf_op jit(solution)/shard_map/all_gather | solution.py:108
  135.8 0.0 copy-start.1
  135.8 0.7 copy-done.1
  136.5 0.0 copy-start.2
  136.5 22.6 %shard_map.86 = f32[8,128,256]{2,1,0:T(8,128)S(1)} custom-call(s32[8,64]{1,0:T(8,128)S(1)} %copy-done.1, s32[8,1]{1,0:T(8,128)S(1)} %copy.9.counts_ref, bf16[8,64,128,128]{3,2,1,0:T(8,128)(2,1)} %values_ref.1, bf16[256,128,256]{2,1,0:T(8,128)(2,1)} %bitcast.39), custom_call_target="tpu_custom_call" | custom-call | flops 4294967296 | bytes 34603008 | tf_op jit(solution)/shard_map/pallas_call | solution.py:90
  159.1 0.0 copy-done
  159.1 0.8 convolution_multiply_fusion
  159.9 0.1 collective-permute-start.1
  160.0 1.3 collective-permute-done.1
  161.3 1.6 collective-permute-start.4
  162.9 0.0 collective-permute-start.3
  162.9 1.8 collective-permute-start.2
  164.7 1.3 collective-permute-start
  166.0 3.6 %collective-permute-done.4 = f32[128,256]{1,0:T(8,128)S(1)} collective-permute-done((f32[128,256]{1,0:T(8,128)S(1)}, f32[128,256]{1,0:T(8,128)S(1)}, u32[]{:S(2)}, u32[]{:S(2)}) %collective-permute-start.4) | collective-permute-done | bytes 131104 | tf_op jit(solution)/shard_map/ppermute | solution.py:40
  169.7 0.0 collective-permute-done.3
  169.7 1.0 collective-permute-done.2
  170.7 0.6 gather_fusion
  171.3 0.1 broadcast_select_fusion.2
  171.5 2.0 collective-permute-start.7
  173.5 1.6 collective-permute-start.6
  175.1 0.0 collective-permute-start.5
  175.2 1.8 collective-permute-done.7
  177.0 2.2 %collective-permute-done.6 = f32[128,256]{1,0:T(8,128)S(1)} collective-permute-done((f32[128,256]{1,0:T(8,128)S(1)}, f32[128,256]{1,0:T(8,128)S(1)}, u32[]{:S(2)}, u32[]{:S(2)}) %collective-permute-start.6) | collective-permute-done | bytes 131104 | tf_op jit(solution)/shard_map/ppermute | solution.py:40
  179.2 0.4 collective-permute-done.5
  179.7 0.6 gather_fusion.1
  180.3 0.1 broadcast_select_fusion.1
  180.4 0.8 collective-permute-start.10
  181.2 1.4 collective-permute-start.9
  182.7 1.1 collective-permute-start.8
  183.8 3.1 %collective-permute-done.10 = f32[128,256]{1,0:T(8,128)S(1)} collective-permute-done((f32[128,256]{1,0:T(8,128)S(1)}, f32[128,256]{1,0:T(8,128)S(1)}, u32[]{:S(2)}, u32[]{:S(2)}) %collective-permute-start.10) | collective-permute-done | bytes 131104 | tf_op jit(solution)/shard_map/ppermute | solution.py:40
  186.9 0.0 collective-permute-done.9
  186.9 0.6 collective-permute-done.8
  187.6 0.6 gather_fusion.2
  188.2 0.1 broadcast_select_fusion
  188.3 5.1 %collective-permute-start.11 = (f32[128,256]{1,0:T(8,128)S(1)}, f32[128,256]{1,0:T(8,128)S(1)}, u32[]{:S(2)}, u32[]{:S(2)}) collective-permute-start(f32[128,256]{1,0:T(8,128)S(1)} %fusion.4), channel_id=1, source_target_pairs={{0,2},{1,3},{2,0},{3,1},{4,6},{5,7},{6,4},{7,5},{8,10},{9,11},{10,... | collective-permute-start | bytes 393224 | tf_op jit(solution)/shard_map/ppermute | solution.py:46
  193.4 0.0 collective-permute-done
  193.4 0.0 copy-done.2
  193.4 2.0 convolution_convert_fusion
  195.4 0.0 collective-permute-done.11
  195.4 0.7 maximum_select_fusion
  (19 shorter events, 0.4 us)
Async XLA Ops:
  7.2 151.9 %copy-start = (bf16[1024,256]{1,0:T(8,128)(2,1)S(1)}, bf16[1024,256]{1,0:T(8,128)(2,1)}, u32[]{:S(2)}) copy-start(bf16[1024,256]{1,0:T(8,128)(2,1)} %param.15) | copy-start | bytes 1572868
  7.2 128.6 %all-gather.2.cloned.1.call-start = ((), (), s32[]{:S(2)}) async-start(), calls=%async_computation | async-start | bytes 17039360 | tf_op jit(solution)/shard_map/all_gather | solution.py:108
  135.8 0.7 copy-start.1
  136.5 56.9 %copy-start.2 = (bf16[256,256]{1,0:T(8,128)(2,1)S(1)}, bf16[256,256]{1,0:T(8,128)(2,1)}, u32[]{:S(2)}) copy-start(bf16[256,256]{1,0:T(8,128)(2,1)} %param.16) | copy-start | bytes 393220
  159.9 1.4 collective-permute-start.1
  161.3 8.3 %collective-permute-start.4 = (f32[128,256]{1,0:T(8,128)S(1)}, f32[128,256]{1,0:T(8,128)S(1)}, u32[]{:S(2)}, u32[]{:S(2)}) collective-permute-start(f32[128,256]{1,0:T(8,128)S(1)} %bitcast_add_fusion.1), channel_id=1, source_target_pairs={{0,5},{1,4},{2,7},{3,6},{4,1},{5,0},{6,3},{7,2},{8,13},{9,12},{10,... | collective-permute-start | bytes 393224 | tf_op jit(solution)/shard_map/ppermute | solution.py:40
  162.9 6.8 %collective-permute-start.3 = (f32[128,256]{1,0:T(8,128)S(1)}, f32[128,256]{1,0:T(8,128)S(1)}, u32[]{:S(2)}, u32[]{:S(2)}) collective-permute-start(f32[128,256]{1,0:T(8,128)S(1)} %bitcast_add_fusion.1), channel_id=1, source_target_pairs={{0,1},{1,0},{2,3},{3,2},{4,5},{5,4},{6,7},{7,6},{8,9},{9,8},{10,11... | collective-permute-start | bytes 393224 | tf_op jit(solution)/shard_map/ppermute | solution.py:40
  162.9 7.8 %collective-permute-start.2 = (f32[128,256]{1,0:T(8,128)S(1)}, f32[128,256]{1,0:T(8,128)S(1)}, u32[]{:S(2)}, u32[]{:S(2)}) collective-permute-start(f32[128,256]{1,0:T(8,128)S(1)} %bitcast_add_fusion.1), channel_id=1, source_target_pairs={{0,4},{1,5},{2,6},{3,7},{4,0},{5,1},{6,2},{7,3},{8,12},{9,13},{10,... | collective-permute-start | bytes 393224 | tf_op jit(solution)/shard_map/ppermute | solution.py:40
  164.7 28.7 %collective-permute-start = (f32[512,256]{1,0:T(8,128)S(1)}, f32[512,256]{1,0:T(8,128)}, u32[]{:S(2)}, u32[]{:S(2)}) collective-permute-start(f32[512,256]{1,0:T(8,128)S(1)} %select_bitcast_fusion), channel_id=1, source_target_pairs={{0,1},{1,0},{2,3},{3,2},{4,5},{5,4},{6,7},{7,6},{8,9},{9,8},{10,11... | collective-permute-start | bytes 1572872 | tf_op jit(solution)/shard_map/ppermute | solution.py:120
  171.5 5.5 %collective-permute-start.7 = (f32[128,256]{1,0:T(8,128)S(1)}, f32[128,256]{1,0:T(8,128)S(1)}, u32[]{:S(2)}, u32[]{:S(2)}) collective-permute-start(f32[128,256]{1,0:T(8,128)S(1)} %fusion.11), channel_id=1, source_target_pairs={{0,24},{1,25},{2,26},{3,27},{4,28},{5,29},{6,30},{7,31},{8,16},{9,... | collective-permute-start | bytes 393224 | tf_op jit(solution)/shard_map/ppermute | solution.py:40
  173.5 5.7 %collective-permute-start.6 = (f32[128,256]{1,0:T(8,128)S(1)}, f32[128,256]{1,0:T(8,128)S(1)}, u32[]{:S(2)}, u32[]{:S(2)}) collective-permute-start(f32[128,256]{1,0:T(8,128)S(1)} %fusion.11), channel_id=1, source_target_pairs={{0,16},{1,17},{2,18},{3,19},{4,20},{5,21},{6,22},{7,23},{8,24},{9,... | collective-permute-start | bytes 393224 | tf_op jit(solution)/shard_map/ppermute | solution.py:40
  175.1 4.5 %collective-permute-start.5 = (f32[128,256]{1,0:T(8,128)S(1)}, f32[128,256]{1,0:T(8,128)S(1)}, u32[]{:S(2)}, u32[]{:S(2)}) collective-permute-start(f32[128,256]{1,0:T(8,128)S(1)} %fusion.11), channel_id=1, source_target_pairs={{0,8},{1,9},{2,10},{3,11},{4,12},{5,13},{6,14},{7,15},{8,0},{9,1},... | collective-permute-start | bytes 393224 | tf_op jit(solution)/shard_map/ppermute | solution.py:40
  180.4 6.5 %collective-permute-start.10 = (f32[128,256]{1,0:T(8,128)S(1)}, f32[128,256]{1,0:T(8,128)S(1)}, u32[]{:S(2)}, u32[]{:S(2)}) collective-permute-start(f32[128,256]{1,0:T(8,128)S(1)} %fusion.10), channel_id=1, source_target_pairs={{0,96},{1,97},{2,98},{3,99},{4,100},{5,101},{6,102},{7,103},{8,104... | collective-permute-start | bytes 393224 | tf_op jit(solution)/shard_map/ppermute | solution.py:40
  181.2 5.7 %collective-permute-start.9 = (f32[128,256]{1,0:T(8,128)S(1)}, f32[128,256]{1,0:T(8,128)S(1)}, u32[]{:S(2)}, u32[]{:S(2)}) collective-permute-start(f32[128,256]{1,0:T(8,128)S(1)} %fusion.10), channel_id=1, source_target_pairs={{0,64},{1,65},{2,66},{3,67},{4,68},{5,69},{6,70},{7,71},{8,72},{9,... | collective-permute-start | bytes 393224 | tf_op jit(solution)/shard_map/ppermute | solution.py:40
  182.7 4.9 %collective-permute-start.8 = (f32[128,256]{1,0:T(8,128)S(1)}, f32[128,256]{1,0:T(8,128)S(1)}, u32[]{:S(2)}, u32[]{:S(2)}) collective-permute-start(f32[128,256]{1,0:T(8,128)S(1)} %fusion.10), channel_id=1, source_target_pairs={{0,32},{1,33},{2,34},{3,35},{4,36},{5,37},{6,38},{7,39},{8,40},{9,... | collective-permute-start | bytes 393224 | tf_op jit(solution)/shard_map/ppermute | solution.py:40
  188.3 7.1 %collective-permute-start.11 = (f32[128,256]{1,0:T(8,128)S(1)}, f32[128,256]{1,0:T(8,128)S(1)}, u32[]{:S(2)}, u32[]{:S(2)}) collective-permute-start(f32[128,256]{1,0:T(8,128)S(1)} %fusion.4), channel_id=1, source_target_pairs={{0,2},{1,3},{2,0},{3,1},{4,6},{5,7},{6,4},{7,5},{8,10},{9,11},{10,... | collective-permute-start | bytes 393224 | tf_op jit(solution)/shard_map/ppermute | solution.py:46
Sparse Core Ops, SparseCore 0:
  10.3 125.4 all-gather.1

commit v5 on v3

--- a/solution.py
+++ b/solution.py
@@ -9,7 +9,7 @@
 
 AXES = ("row", "rep")
 CORE_BIT = 1
-DOUBLING_STAGES = ((2, 0), (3, 4), (5, 6))
+DOUBLING_STAGES = ((2,), (3,), (4,), (5,), (6,), (0,))
 
 
 def xor_pairs(count, mask):

time: 200 us -> 209 us (1.045)
  waiting for transfers between devices: 138 us -> 143 us
  starting transfers between devices: 20.8 us -> 25.3 us
    ppermute x9 -> x6, waiting for transfers between devices: 11.4 us -> 16.3 us  [butterfly_sum(): lax.ppermute(buf, AXES, xor_pairs(count, group_mask(d, bits)))]
    ppermute x1, starting transfers between devices: 3.45 us -> 0.37 us  [butterfly_sum(): lax.ppermute(jnp.take(parts, 1 - core, axis=0), AXES, xor_pairs(count, co...]
    ppermute x1, starting transfers between devices: 4.66 us -> 7.41 us  [butterfly_sum(): got = lax.ppermute(buf, AXES, xor_pairs(count, core_mask))]
    ppermute x9 -> x6, starting transfers between devices: 10.2 us -> 12.8 us  [butterfly_sum(): lax.ppermute(buf, AXES, xor_pairs(count, group_mask(d, bits)))]
    ppermute x1, starting transfers between devices: 2.41 us -> 4.7 us  [shards(): lax.ppermute(jnp.take(halves, 1 - rep, axis=0), 'rep', [(0, 1), (1, 0)])]
  transfers between devices with their start and end apart: 13 -> 10, of which waited for: 9 -> 7; matrix products, arithmetic and copies ran while one was open for 3% -> 3% of each run, Pallas kernels for 0% -> 0%
where the time goes in v5:
time: 209 us; the launch traced here: 208 us
  waiting for transfers between devices  143 us (68%)
  starting transfers between devices  25.3 us (12%)
  Pallas kernels  14.8 us (7%)
  between operations  14.3 us (7%)
  local copies, waits for them, and re-layouts  4.83 us (2%)
  other arithmetic  3.66 us (2%)
    all_gather x1, waiting for transfers between devices, shards(): gathered = lax.all_gather(gated, 'row', axis=0, tiled=True)  126 us
    ppermute x6, waiting for transfers between devices, butterfly_sum(): lax.ppermute(buf, AXES, xor_pairs(count, group_mask(d, bits)))  16.3 us
    pallas_call x1, Pallas kernels, propagate_tiles(): pl.pallas_call(tile_kernel, out_shape=jax.ShapeDtypeStruct((row_tiles, ti...  14.8 us
    ppermute x6, starting transfers between devices, butterfly_sum(): lax.ppermute(buf, AXES, xor_pairs(count, group_mask(d, bits)))  12.8 us
    ppermute x1, starting transfers between devices, butterfly_sum(): got = lax.ppermute(buf, AXES, xor_pairs(count, core_mask))  7.41 us
    ppermute x1, starting transfers between devices, shards(): lax.ppermute(jnp.take(halves, 1 - rep, axis=0), 'rep', [(0, 1), (1, 0)])  4.7 us
  transfers between devices with their start and end apart: 10, of which 7 were waited for; matrix products, arithmetic and copies ran while one was open for 3% of the time, Pallas kernels for 0%

profile of v5, /device:TPU:1, one launch (start us, length us, event | category | flops | bytes accessed | tf_op | source)
XLA Modules:
  0.0 207.7 jit_solution(15471955447038010651)
XLA Ops:
  7.2 0.0 copy-start
  7.2 0.0 all-gather.2.cloned.1.call-start
  7.2 1.9 convert_multiply_fusion
  9.2 0.0 all-gather.2.cloned.1.call-update
  9.2 0.7 copy.9.counts_ref
  10.1 125.7 %all-gather.2.cloned.1.call-done = bf16[32768,256]{1,0:T(8,128)(2,1)} async-done(((bf16[512,256]{1,0:T(8,128)(2,1)}), bf16[32768,256]{1,0:T(8,128)(2,1)}) %all-gather.2.cloned.1.call-update) | async-done | bytes 16777232 | tf_op jit(solution)/shard_map/all_gather | solution.py:108
  135.8 0.0 copy-start.1
  135.8 0.7 copy-done.1
  136.5 14.8 %shard_map.86 = f32[8,128,256]{2,1,0:T(8,128)S(1)} custom-call(s32[8,64]{1,0:T(8,128)S(1)} %copy-done.1, s32[8,1]{1,0:T(8,128)S(1)} %copy.9.counts_ref, bf16[8,64,128,128]{3,2,1,0:T(8,128)(2,1)} %values_ref.1, bf16[256,128,256]{2,1,0:T(8,128)(2,1)} %bitcast.42), custom_call_target="tpu_custom_call" | custom-call | flops 4294967296 | bytes 34603008 | tf_op jit(solution)/shard_map/pallas_call | solution.py:90
  151.2 0.0 copy-start.2
  151.3 0.0 copy-done
  151.3 0.8 convolution_multiply_fusion
  152.1 0.4 collective-permute-start.1
  152.5 1.0 collective-permute-done.1
  153.5 2.6 %collective-permute-start.2 = (f32[128,256]{1,0:T(8,128)S(1)}, f32[128,256]{1,0:T(8,128)S(1)}, u32[]{:S(2)}, u32[]{:S(2)}) collective-permute-start(f32[128,256]{1,0:T(8,128)S(1)} %bitcast_add_fusion.1), channel_id=1, source_target_pairs={{0,4},{1,5},{2,6},{3,7},{4,0},{5,1},{6,2},{7,3},{8,12},{9,13},{10,... | collective-permute-start | bytes 393224 | tf_op jit(solution)/shard_map/ppermute | solution.py:40
  156.2 4.7 %collective-permute-start = (f32[512,256]{1,0:T(8,128)S(1)}, f32[512,256]{1,0:T(8,128)S(1)}, u32[]{:S(2)}, u32[]{:S(2)}) collective-permute-start(f32[512,256]{1,0:T(8,128)S(1)} %select_bitcast_fusion), channel_id=1, source_target_pairs={{0,1},{1,0},{2,3},{3,2},{4,5},{5,4},{6,7},{7,6},{8,9},{9,8},{10,11... | collective-permute-start | bytes 1572872 | tf_op jit(solution)/shard_map/ppermute | solution.py:120
  160.9 0.0 collective-permute-done.2
  160.9 0.6 gather_fusion
  161.5 0.1 broadcast_select_fusion.5
  161.6 3.3 %collective-permute-start.3 = (f32[128,256]{1,0:T(8,128)S(1)}, f32[128,256]{1,0:T(8,128)S(1)}, u32[]{:S(2)}, u32[]{:S(2)}) collective-permute-start(f32[128,256]{1,0:T(8,128)S(1)} %fusion.14), channel_id=1, source_target_pairs={{0,8},{1,9},{2,10},{3,11},{4,12},{5,13},{6,14},{7,15},{8,0},{9,1},... | collective-permute-start | bytes 393224 | tf_op jit(solution)/shard_map/ppermute | solution.py:40
  165.0 2.8 %collective-permute-done.3 = f32[128,256]{1,0:T(8,128)S(1)} collective-permute-done((f32[128,256]{1,0:T(8,128)S(1)}, f32[128,256]{1,0:T(8,128)S(1)}, u32[]{:S(2)}, u32[]{:S(2)}) %collective-permute-start.3) | collective-permute-done | bytes 131104 | tf_op jit(solution)/shard_map/ppermute | solution.py:40
  167.8 0.6 gather_fusion.1
  168.4 0.1 broadcast_select_fusion.4
  168.5 1.2 collective-permute-start.4
  169.7 4.5 %collective-permute-done.4 = f32[128,256]{1,0:T(8,128)S(1)} collective-permute-done((f32[128,256]{1,0:T(8,128)S(1)}, f32[128,256]{1,0:T(8,128)S(1)}, u32[]{:S(2)}, u32[]{:S(2)}) %collective-permute-start.4) | collective-permute-done | bytes 131104 | tf_op jit(solution)/shard_map/ppermute | solution.py:40
  174.2 0.6 gather_fusion.2
  174.8 0.1 broadcast_select_fusion.3
  174.9 0.5 collective-permute-start.5
  175.4 3.4 %collective-permute-done.5 = f32[128,256]{1,0:T(8,128)S(1)} collective-permute-done((f32[128,256]{1,0:T(8,128)S(1)}, f32[128,256]{1,0:T(8,128)S(1)}, u32[]{:S(2)}, u32[]{:S(2)}) %collective-permute-start.5) | collective-permute-done | bytes 131104 | tf_op jit(solution)/shard_map/ppermute | solution.py:40
  178.8 0.6 gather_fusion.3
  179.4 0.1 broadcast_select_fusion.2
  179.5 2.5 %collective-permute-start.6 = (f32[128,256]{1,0:T(8,128)S(1)}, f32[128,256]{1,0:T(8,128)S(1)}, u32[]{:S(2)}, u32[]{:S(2)}) collective-permute-start(f32[128,256]{1,0:T(8,128)S(1)} %fusion.11), channel_id=1, source_target_pairs={{0,64},{1,65},{2,66},{3,67},{4,68},{5,69},{6,70},{7,71},{8,72},{9,... | collective-permute-start | bytes 393224 | tf_op jit(solution)/shard_map/ppermute | solution.py:40
  182.1 2.8 %collective-permute-done.6 = f32[128,256]{1,0:T(8,128)S(1)} collective-permute-done((f32[128,256]{1,0:T(8,128)S(1)}, f32[128,256]{1,0:T(8,128)S(1)}, u32[]{:S(2)}, u32[]{:S(2)}) %collective-permute-start.6) | collective-permute-done | bytes 131104 | tf_op jit(solution)/shard_map/ppermute | solution.py:40
  185.0 0.6 gather_fusion.4
  185.5 0.1 broadcast_select_fusion.1
  185.6 2.6 %collective-permute-start.7 = (f32[128,256]{1,0:T(8,128)S(1)}, f32[128,256]{1,0:T(8,128)S(1)}, u32[]{:S(2)}, u32[]{:S(2)}) collective-permute-start(f32[128,256]{1,0:T(8,128)S(1)} %fusion.10), channel_id=1, source_target_pairs={{0,1},{1,0},{2,3},{3,2},{4,5},{5,4},{6,7},{7,6},{8,9},{9,8},{10,11... | collective-permute-start | bytes 393224 | tf_op jit(solution)/shard_map/ppermute | solution.py:40
  188.3 2.8 %collective-permute-done.7 = f32[128,256]{1,0:T(8,128)S(1)} collective-permute-done((f32[128,256]{1,0:T(8,128)S(1)}, f32[128,256]{1,0:T(8,128)S(1)}, u32[]{:S(2)}, u32[]{:S(2)}) %collective-permute-start.7) | collective-permute-done | bytes 131104 | tf_op jit(solution)/shard_map/ppermute | solution.py:40
  191.1 0.6 gather_fusion.5
  191.6 0.1 broadcast_select_fusion
  191.8 7.4 %collective-permute-start.8 = (f32[128,256]{1,0:T(8,128)S(1)}, f32[128,256]{1,0:T(8,128)S(1)}, u32[]{:S(2)}, u32[]{:S(2)}) collective-permute-start(f32[128,256]{1,0:T(8,128)S(1)} %fusion.4), channel_id=1, source_target_pairs={{0,2},{1,3},{2,0},{3,1},{4,6},{5,7},{6,4},{7,5},{8,10},{9,11},{10,... | collective-permute-start | bytes 393224 | tf_op jit(solution)/shard_map/ppermute | solution.py:46
  199.2 0.0 collective-permute-done
  199.2 0.0 copy-done.2
  199.2 1.0 convolution_convert_fusion
  200.2 0.0 collective-permute-done.8
  200.2 0.7 maximum_select_fusion
  (35 shorter events, 0.5 us)
Async XLA Ops:
  7.2 144.1 %copy-start = (bf16[1024,256]{1,0:T(8,128)(2,1)S(1)}, bf16[1024,256]{1,0:T(8,128)(2,1)}, u32[]{:S(2)}) copy-start(bf16[1024,256]{1,0:T(8,128)(2,1)} %param.15) | copy-start | bytes 1572868
  7.2 128.6 %all-gather.2.cloned.1.call-start = ((), (), s32[]{:S(2)}) async-start(), calls=%async_computation | async-start | bytes 17039360 | tf_op jit(solution)/shard_map/all_gather | solution.py:108
  135.8 0.7 copy-start.1
  151.2 47.9 %copy-start.2 = (bf16[256,256]{1,0:T(8,128)(2,1)S(1)}, bf16[256,256]{1,0:T(8,128)(2,1)}, u32[]{:S(2)}) copy-start(bf16[256,256]{1,0:T(8,128)(2,1)} %param.16) | copy-start | bytes 393220
  152.1 1.4 collective-permute-start.1
  153.5 7.4 %collective-permute-start.2 = (f32[128,256]{1,0:T(8,128)S(1)}, f32[128,256]{1,0:T(8,128)S(1)}, u32[]{:S(2)}, u32[]{:S(2)}) collective-permute-start(f32[128,256]{1,0:T(8,128)S(1)} %bitcast_add_fusion.1), channel_id=1, source_target_pairs={{0,4},{1,5},{2,6},{3,7},{4,0},{5,1},{6,2},{7,3},{8,12},{9,13},{10,... | collective-permute-start | bytes 393224 | tf_op jit(solution)/shard_map/ppermute | solution.py:40
  156.2 43.0 %collective-permute-start = (f32[512,256]{1,0:T(8,128)S(1)}, f32[512,256]{1,0:T(8,128)S(1)}, u32[]{:S(2)}, u32[]{:S(2)}) collective-permute-start(f32[512,256]{1,0:T(8,128)S(1)} %select_bitcast_fusion), channel_id=1, source_target_pairs={{0,1},{1,0},{2,3},{3,2},{4,5},{5,4},{6,7},{7,6},{8,9},{9,8},{10,11... | collective-permute-start | bytes 1572872 | tf_op jit(solution)/shard_map/ppermute | solution.py:120
  161.6 6.2 %collective-permute-start.3 = (f32[128,256]{1,0:T(8,128)S(1)}, f32[128,256]{1,0:T(8,128)S(1)}, u32[]{:S(2)}, u32[]{:S(2)}) collective-permute-start(f32[128,256]{1,0:T(8,128)S(1)} %fusion.14), channel_id=1, source_target_pairs={{0,8},{1,9},{2,10},{3,11},{4,12},{5,13},{6,14},{7,15},{8,0},{9,1},... | collective-permute-start | bytes 393224 | tf_op jit(solution)/shard_map/ppermute | solution.py:40
  168.5 5.7 %collective-permute-start.4 = (f32[128,256]{1,0:T(8,128)S(1)}, f32[128,256]{1,0:T(8,128)S(1)}, u32[]{:S(2)}, u32[]{:S(2)}) collective-permute-start(f32[128,256]{1,0:T(8,128)S(1)} %fusion.13), channel_id=1, source_target_pairs={{0,16},{1,17},{2,18},{3,19},{4,20},{5,21},{6,22},{7,23},{8,24},{9,... | collective-permute-start | bytes 393224 | tf_op jit(solution)/shard_map/ppermute | solution.py:40
  174.9 3.9 %collective-permute-start.5 = (f32[128,256]{1,0:T(8,128)S(1)}, f32[128,256]{1,0:T(8,128)S(1)}, u32[]{:S(2)}, u32[]{:S(2)}) collective-permute-start(f32[128,256]{1,0:T(8,128)S(1)} %fusion.12), channel_id=1, source_target_pairs={{0,32},{1,33},{2,34},{3,35},{4,36},{5,37},{6,38},{7,39},{8,40},{9,... | collective-permute-start | bytes 393224 | tf_op jit(solution)/shard_map/ppermute | solution.py:40
  179.5 5.4 %collective-permute-start.6 = (f32[128,256]{1,0:T(8,128)S(1)}, f32[128,256]{1,0:T(8,128)S(1)}, u32[]{:S(2)}, u32[]{:S(2)}) collective-permute-start(f32[128,256]{1,0:T(8,128)S(1)} %fusion.11), channel_id=1, source_target_pairs={{0,64},{1,65},{2,66},{3,67},{4,68},{5,69},{6,70},{7,71},{8,72},{9,... | collective-permute-start | bytes 393224 | tf_op jit(solution)/shard_map/ppermute | solution.py:40
  185.6 5.4 %collective-permute-start.7 = (f32[128,256]{1,0:T(8,128)S(1)}, f32[128,256]{1,0:T(8,128)S(1)}, u32[]{:S(2)}, u32[]{:S(2)}) collective-permute-start(f32[128,256]{1,0:T(8,128)S(1)} %fusion.10), channel_id=1, source_target_pairs={{0,1},{1,0},{2,3},{3,2},{4,5},{5,4},{6,7},{7,6},{8,9},{9,8},{10,11... | collective-permute-start | bytes 393224 | tf_op jit(solution)/shard_map/ppermute | solution.py:40
  191.8 8.4 %collective-permute-start.8 = (f32[128,256]{1,0:T(8,128)S(1)}, f32[128,256]{1,0:T(8,128)S(1)}, u32[]{:S(2)}, u32[]{:S(2)}) collective-permute-start(f32[128,256]{1,0:T(8,128)S(1)} %fusion.4), channel_id=1, source_target_pairs={{0,2},{1,3},{2,0},{3,1},{4,6},{5,7},{6,4},{7,5},{8,10},{9,11},{10,... | collective-permute-start | bytes 393224 | tf_op jit(solution)/shard_map/ppermute | solution.py:46
Sparse Core Ops, SparseCore 0:
  10.3 125.4 all-gather.1

commit v6 on v5

--- a/solution.py
+++ b/solution.py
@@ -9,7 +9,7 @@
 
 AXES = ("row", "rep")
 CORE_BIT = 1
-DOUBLING_STAGES = ((2,), (3,), (4,), (5,), (6,), (0,))
+DOUBLING_STAGES = ((3, 4), (5, 6), (2, 0))
 
 
 def xor_pairs(count, mask):

time: 209 us -> 200 us (0.957)
  starting transfers between devices: 25.3 us -> 21.3 us
  waiting for transfers between devices: 143 us -> 139 us
    ppermute x1, starting transfers between devices: 7.41 us -> 3.65 us  [butterfly_sum(): got = lax.ppermute(buf, AXES, xor_pairs(count, core_mask))]
    ppermute x6 -> x9, waiting for transfers between devices: 16.3 us -> 12.6 us  [butterfly_sum(): lax.ppermute(buf, AXES, xor_pairs(count, group_mask(d, bits)))]
    ppermute x6 -> x9, starting transfers between devices: 12.8 us -> 14.5 us  [butterfly_sum(): lax.ppermute(buf, AXES, xor_pairs(count, group_mask(d, bits)))]
  transfers between devices with their start and end apart: 10 -> 13, of which waited for: 7 -> 11; matrix products, arithmetic and copies ran while one was open for 3% -> 3% of each run, Pallas kernels for 0% -> 0%
where the time goes in v6:
time: 200 us; the launch traced here: 199 us
  waiting for transfers between devices  139 us (70%)
  starting transfers between devices  21.3 us (11%)
  Pallas kernels  14.8 us (7%)
  between operations  14.2 us (7%)
  other arithmetic  3.38 us (2%)
  local copies, waits for them, and re-layouts  3.18 us (2%)
  matrix products  2.81 us (1%)
    all_gather x1, waiting for transfers between devices, shards(): gathered = lax.all_gather(gated, 'row', axis=0, tiled=True)  126 us
    pallas_call x1, Pallas kernels, propagate_tiles(): pl.pallas_call(tile_kernel, out_shape=jax.ShapeDtypeStruct((row_tiles, ti...  14.8 us
    ppermute x9, starting transfers between devices, butterfly_sum(): lax.ppermute(buf, AXES, xor_pairs(count, group_mask(d, bits)))  14.5 us
    ppermute x9, waiting for transfers between devices, butterfly_sum(): lax.ppermute(buf, AXES, xor_pairs(count, group_mask(d, bits)))  12.6 us
  transfers between devices with their start and end apart: 13, of which 11 were waited for; matrix products, arithmetic and copies ran while one was open for 3% of the time, Pallas kernels for 0%

profile of v6, /device:TPU:1, one launch (start us, length us, event | category | flops | bytes accessed | tf_op | source)
XLA Modules:
  0.0 199.1 jit_solution(8739058084197600946)
XLA Ops:
  7.2 0.0 copy-start
  7.2 0.0 all-gather.2.cloned.1.call-start
  7.2 1.9 convert_multiply_fusion
  9.2 0.0 all-gather.2.cloned.1.call-update
  9.2 0.7 copy.9.counts_ref
  10.0 125.8 %all-gather.2.cloned.1.call-done = bf16[32768,256]{1,0:T(8,128)(2,1)} async-done(((bf16[512,256]{1,0:T(8,128)(2,1)}), bf16[32768,256]{1,0:T(8,128)(2,1)}) %all-gather.2.cloned.1.call-update) | async-done | bytes 16777232 | tf_op jit(solution)/shard_map/all_gather | solution.py:108
  135.8 0.0 copy-start.1
  135.8 0.7 copy-done.1
  136.5 0.0 copy-start.2
  136.5 14.8 %shard_map.86 = f32[8,128,256]{2,1,0:T(8,128)S(1)} custom-call(s32[8,64]{1,0:T(8,128)S(1)} %copy-done.1, s32[8,1]{1,0:T(8,128)S(1)} %copy.9.counts_ref, bf16[8,64,128,128]{3,2,1,0:T(8,128)(2,1)} %values_ref.1, bf16[256,128,256]{2,1,0:T(8,128)(2,1)} %bitcast.39), custom_call_target="tpu_custom_call" | custom-call | flops 4294967296 | bytes 34603008 | tf_op jit(solution)/shard_map/pallas_call | solution.py:90
  151.2 0.0 copy-done
  151.3 0.8 convolution_multiply_fusion
  152.1 0.4 collective-permute-start.1
  152.5 1.0 collective-permute-done.1
  153.5 7.2 %collective-permute-start.4 = (f32[128,256]{1,0:T(8,128)S(1)}, f32[128,256]{1,0:T(8,128)S(1)}, u32[]{:S(2)}, u32[]{:S(2)}) collective-permute-start(f32[128,256]{1,0:T(8,128)S(1)} %bitcast_add_fusion.1), channel_id=1, source_target_pairs={{0,24},{1,25},{2,26},{3,27},{4,28},{5,29},{6,30},{7,31},{8,16},{9,... | collective-permute-start | bytes 393224 | tf_op jit(solution)/shard_map/ppermute | solution.py:40
  160.7 0.0 collective-permute-start.3
  160.7 0.7 collective-permute-start.2
  161.4 2.8 %collective-permute-start = (f32[512,256]{1,0:T(8,128)S(1)}, f32[512,256]{1,0:T(8,128)}, u32[]{:S(2)}, u32[]{:S(2)}) collective-permute-start(f32[512,256]{1,0:T(8,128)S(1)} %select_bitcast_fusion), channel_id=1, source_target_pairs={{0,1},{1,0},{2,3},{3,2},{4,5},{5,4},{6,7},{7,6},{8,9},{9,8},{10,11... | collective-permute-start | bytes 1572872 | tf_op jit(solution)/shard_map/ppermute | solution.py:120
  164.2 2.0 %collective-permute-done.4 = f32[128,256]{1,0:T(8,128)S(1)} collective-permute-done((f32[128,256]{1,0:T(8,128)S(1)}, f32[128,256]{1,0:T(8,128)S(1)}, u32[]{:S(2)}, u32[]{:S(2)}) %collective-permute-start.4) | collective-permute-done | bytes 131104 | tf_op jit(solution)/shard_map/ppermute | solution.py:40
  166.2 0.6 collective-permute-done.3
  166.8 0.9 collective-permute-done.2
  167.8 0.6 gather_fusion
  168.4 0.1 broadcast_select_fusion.2
  168.6 1.7 collective-permute-start.7
  170.3 0.0 collective-permute-start.6
  170.3 1.6 collective-permute-start.5
  171.9 2.1 %collective-permute-done.7 = f32[128,256]{1,0:T(8,128)S(1)} collective-permute-done((f32[128,256]{1,0:T(8,128)S(1)}, f32[128,256]{1,0:T(8,128)S(1)}, u32[]{:S(2)}, u32[]{:S(2)}) %collective-permute-start.7) | collective-permute-done | bytes 131104 | tf_op jit(solution)/shard_map/ppermute | solution.py:40
  174.1 2.0 collective-permute-done.6
  176.0 0.9 collective-permute-done.5
  177.0 0.6 gather_fusion.1
  177.5 0.1 broadcast_select_fusion.1
  177.7 1.3 collective-permute-start.10
  179.0 1.0 collective-permute-start.9
  180.0 1.1 collective-permute-start.8
  181.1 1.7 collective-permute-done.10
  182.8 1.5 collective-permute-done.9
  184.3 0.8 collective-permute-done.8
  185.1 0.6 gather_fusion.2
  185.7 0.1 broadcast_select_fusion
  185.9 3.7 %collective-permute-start.11 = (f32[128,256]{1,0:T(8,128)S(1)}, f32[128,256]{1,0:T(8,128)S(1)}, u32[]{:S(2)}, u32[]{:S(2)}) collective-permute-start(f32[128,256]{1,0:T(8,128)S(1)} %fusion.4), channel_id=1, source_target_pairs={{0,2},{1,3},{2,0},{3,1},{4,6},{5,7},{6,4},{7,5},{8,10},{9,11},{10,... | collective-permute-start | bytes 393224 | tf_op jit(solution)/shard_map/ppermute | solution.py:46
  189.5 0.0 collective-permute-done
  189.5 0.0 copy-done.2
  189.5 2.0 %convolution_convert_fusion = bf16[512,256]{1,0:T(8,128)(2,1)} fusion(bf16[256,256]{1,0:T(8,128)(2,1)S(1)} %copy-done.2, f32[512,256]{1,0:T(8,128)} %collective-permute-done, f32[2,512,256]{2,1,0:T(8,128)S(1)} %bitcast.38, s32[]{:T(128)S(6)} %select_n.46, pred[]{:T(512)S(6)} %and.48), kind=kOutput, calls=%fused_computation.3 | convolution fusion | flops 67633152 | bytes 1441797 | tf_op jit(solution)/shard_map/dot_general | solution.py:122
  191.6 0.0 collective-permute-done.11
  191.6 0.7 maximum_select_fusion
  (19 shorter events, 0.4 us)
Async XLA Ops:
  7.2 144.1 %copy-start = (bf16[1024,256]{1,0:T(8,128)(2,1)S(1)}, bf16[1024,256]{1,0:T(8,128)(2,1)}, u32[]{:S(2)}) copy-start(bf16[1024,256]{1,0:T(8,128)(2,1)} %param.15) | copy-start | bytes 1572868
  7.2 128.6 %all-gather.2.cloned.1.call-start = ((), (), s32[]{:S(2)}) async-start(), calls=%async_computation | async-start | bytes 17039360 | tf_op jit(solution)/shard_map/all_gather | solution.py:108
  135.8 0.7 copy-start.1
  136.5 53.1 %copy-start.2 = (bf16[256,256]{1,0:T(8,128)(2,1)S(1)}, bf16[256,256]{1,0:T(8,128)(2,1)}, u32[]{:S(2)}) copy-start(bf16[256,256]{1,0:T(8,128)(2,1)} %param.16) | copy-start | bytes 393220
  152.1 1.4 collective-permute-start.1
  153.5 12.7 %collective-permute-start.4 = (f32[128,256]{1,0:T(8,128)S(1)}, f32[128,256]{1,0:T(8,128)S(1)}, u32[]{:S(2)}, u32[]{:S(2)}) collective-permute-start(f32[128,256]{1,0:T(8,128)S(1)} %bitcast_add_fusion.1), channel_id=1, source_target_pairs={{0,24},{1,25},{2,26},{3,27},{4,28},{5,29},{6,30},{7,31},{8,16},{9,... | collective-permute-start | bytes 393224 | tf_op jit(solution)/shard_map/ppermute | solution.py:40
  160.7 6.1 %collective-permute-start.3 = (f32[128,256]{1,0:T(8,128)S(1)}, f32[128,256]{1,0:T(8,128)S(1)}, u32[]{:S(2)}, u32[]{:S(2)}) collective-permute-start(f32[128,256]{1,0:T(8,128)S(1)} %bitcast_add_fusion.1), channel_id=1, source_target_pairs={{0,16},{1,17},{2,18},{3,19},{4,20},{5,21},{6,22},{7,23},{8,24},{9,... | collective-permute-start | bytes 393224 | tf_op jit(solution)/shard_map/ppermute | solution.py:40
  160.7 7.1 %collective-permute-start.2 = (f32[128,256]{1,0:T(8,128)S(1)}, f32[128,256]{1,0:T(8,128)S(1)}, u32[]{:S(2)}, u32[]{:S(2)}) collective-permute-start(f32[128,256]{1,0:T(8,128)S(1)} %bitcast_add_fusion.1), channel_id=1, source_target_pairs={{0,8},{1,9},{2,10},{3,11},{4,12},{5,13},{6,14},{7,15},{8,0},{9,1},... | collective-permute-start | bytes 393224 | tf_op jit(solution)/shard_map/ppermute | solution.py:40
  161.4 28.1 %collective-permute-start = (f32[512,256]{1,0:T(8,128)S(1)}, f32[512,256]{1,0:T(8,128)}, u32[]{:S(2)}, u32[]{:S(2)}) collective-permute-start(f32[512,256]{1,0:T(8,128)S(1)} %select_bitcast_fusion), channel_id=1, source_target_pairs={{0,1},{1,0},{2,3},{3,2},{4,5},{5,4},{6,7},{7,6},{8,9},{9,8},{10,11... | collective-permute-start | bytes 1572872 | tf_op jit(solution)/shard_map/ppermute | solution.py:120
  168.6 5.5 %collective-permute-start.7 = (f32[128,256]{1,0:T(8,128)S(1)}, f32[128,256]{1,0:T(8,128)S(1)}, u32[]{:S(2)}, u32[]{:S(2)}) collective-permute-start(f32[128,256]{1,0:T(8,128)S(1)} %fusion.11), channel_id=1, source_target_pairs={{0,96},{1,97},{2,98},{3,99},{4,100},{5,101},{6,102},{7,103},{8,104... | collective-permute-start | bytes 393224 | tf_op jit(solution)/shard_map/ppermute | solution.py:40
  170.3 5.8 %collective-permute-start.6 = (f32[128,256]{1,0:T(8,128)S(1)}, f32[128,256]{1,0:T(8,128)S(1)}, u32[]{:S(2)}, u32[]{:S(2)}) collective-permute-start(f32[128,256]{1,0:T(8,128)S(1)} %fusion.11), channel_id=1, source_target_pairs={{0,64},{1,65},{2,66},{3,67},{4,68},{5,69},{6,70},{7,71},{8,72},{9,... | collective-permute-start | bytes 393224 | tf_op jit(solution)/shard_map/ppermute | solution.py:40
  170.3 6.7 %collective-permute-start.5 = (f32[128,256]{1,0:T(8,128)S(1)}, f32[128,256]{1,0:T(8,128)S(1)}, u32[]{:S(2)}, u32[]{:S(2)}) collective-permute-start(f32[128,256]{1,0:T(8,128)S(1)} %fusion.11), channel_id=1, source_target_pairs={{0,32},{1,33},{2,34},{3,35},{4,36},{5,37},{6,38},{7,39},{8,40},{9,... | collective-permute-start | bytes 393224 | tf_op jit(solution)/shard_map/ppermute | solution.py:40
  177.7 5.1 %collective-permute-start.10 = (f32[128,256]{1,0:T(8,128)S(1)}, f32[128,256]{1,0:T(8,128)S(1)}, u32[]{:S(2)}, u32[]{:S(2)}) collective-permute-start(f32[128,256]{1,0:T(8,128)S(1)} %fusion.10), channel_id=1, source_target_pairs={{0,5},{1,4},{2,7},{3,6},{4,1},{5,0},{6,3},{7,2},{8,13},{9,12},{10,... | collective-permute-start | bytes 393224 | tf_op jit(solution)/shard_map/ppermute | solution.py:40
  179.0 5.3 %collective-permute-start.9 = (f32[128,256]{1,0:T(8,128)S(1)}, f32[128,256]{1,0:T(8,128)S(1)}, u32[]{:S(2)}, u32[]{:S(2)}) collective-permute-start(f32[128,256]{1,0:T(8,128)S(1)} %fusion.10), channel_id=1, source_target_pairs={{0,1},{1,0},{2,3},{3,2},{4,5},{5,4},{6,7},{7,6},{8,9},{9,8},{10,11... | collective-permute-start | bytes 393224 | tf_op jit(solution)/shard_map/ppermute | solution.py:40
  180.0 5.1 %collective-permute-start.8 = (f32[128,256]{1,0:T(8,128)S(1)}, f32[128,256]{1,0:T(8,128)S(1)}, u32[]{:S(2)}, u32[]{:S(2)}) collective-permute-start(f32[128,256]{1,0:T(8,128)S(1)} %fusion.10), channel_id=1, source_target_pairs={{0,4},{1,5},{2,6},{3,7},{4,0},{5,1},{6,2},{7,3},{8,12},{9,13},{10,... | collective-permute-start | bytes 393224 | tf_op jit(solution)/shard_map/ppermute | solution.py:40
  185.9 5.7 %collective-permute-start.11 = (f32[128,256]{1,0:T(8,128)S(1)}, f32[128,256]{1,0:T(8,128)S(1)}, u32[]{:S(2)}, u32[]{:S(2)}) collective-permute-start(f32[128,256]{1,0:T(8,128)S(1)} %fusion.4), channel_id=1, source_target_pairs={{0,2},{1,3},{2,0},{3,1},{4,6},{5,7},{6,4},{7,5},{8,10},{9,11},{10,... | collective-permute-start | bytes 393224 | tf_op jit(solution)/shard_map/ppermute | solution.py:46
Sparse Core Ops, SparseCore 0:
  10.3 125.4 all-gather.1

commit v7 on v4

--- a/solution.py
+++ b/solution.py
@@ -47,7 +47,7 @@
     return jnp.where(core == 0, jnp.concatenate([buf, got]), jnp.concatenate([got, buf]))
 
 
-SLOT_GROUP = 8
+SLOT_GROUP = 32
 
 
 def tile_kernel(cols_ref, counts_ref, values_ref, grad_ref, out_ref):

time: 203 us -> 199 us (0.980)
  Pallas kernels: 22.6 us -> 15.9 us
  starting transfers between devices: 16.8 us -> 19 us
    pallas_call x1, Pallas kernels: 22.6 us -> 15.9 us  [propagate_tiles(): pl.pallas_call(tile_kernel, out_shape=jax.ShapeDtypeStruct((row_tiles, ti...]
    ppermute x9, starting transfers between devices: 10.3 us -> 12.4 us  [butterfly_sum(): lax.ppermute(buf, AXES, xor_pairs(count, group_mask(d, bits)))]
  transfers between devices with their start and end apart: 13 -> 13, of which waited for: 9 -> 10; matrix products, arithmetic and copies ran while one was open for 3% -> 3% of each run, Pallas kernels for 0% -> 0%
where the time goes in v7:
time: 199 us; the launch traced here: 198 us
  waiting for transfers between devices  139 us (70%)
  starting transfers between devices  19 us (10%)
  Pallas kernels  15.9 us (8%)
  between operations  14.2 us (7%)
  other arithmetic  3.38 us (2%)
  local copies, waits for them, and re-layouts  3.18 us (2%)
  matrix products  2.81 us (1%)
    all_gather x1, waiting for transfers between devices, shards(): gathered = lax.all_gather(gated, 'row', axis=0, tiled=True)  126 us
    pallas_call x1, Pallas kernels, propagate_tiles(): pl.pallas_call(tile_kernel, out_shape=jax.ShapeDtypeStruct((row_tiles, ti...  15.9 us
    ppermute x9, waiting for transfers between devices, butterfly_sum(): lax.ppermute(buf, AXES, xor_pairs(count, group_mask(d, bits)))  12.5 us
    ppermute x9, starting transfers between devices, butterfly_sum(): lax.ppermute(buf, AXES, xor_pairs(count, group_mask(d, bits)))  12.4 us
  transfers between devices with their start and end apart: 13, of which 10 were waited for; matrix products, arithmetic and copies ran while one was open for 3% of the time, Pallas kernels for 0%

profile of v7, /device:TPU:1, one launch (start us, length us, event | category | flops | bytes accessed | tf_op | source)
XLA Modules:
  0.0 197.9 jit_solution(3373962998866367993)
XLA Ops:
  7.2 0.0 copy-start
  7.2 0.0 all-gather.2.cloned.1.call-start
  7.2 1.9 convert_multiply_fusion
  9.2 0.0 all-gather.2.cloned.1.call-update
  9.2 0.7 copy.9.counts_ref
  10.0 125.8 %all-gather.2.cloned.1.call-done = bf16[32768,256]{1,0:T(8,128)(2,1)} async-done(((bf16[512,256]{1,0:T(8,128)(2,1)}), bf16[32768,256]{1,0:T(8,128)(2,1)}) %all-gather.2.cloned.1.call-update) | async-done | bytes 16777232 | tf_op jit(solution)/shard_map/all_gather | solution.py:108
  135.8 0.0 copy-start.1
  135.8 0.7 copy-done.1
  136.5 0.0 copy-start.2
  136.5 15.9 %shard_map.86 = f32[8,128,256]{2,1,0:T(8,128)S(1)} custom-call(s32[8,64]{1,0:T(8,128)S(1)} %copy-done.1, s32[8,1]{1,0:T(8,128)S(1)} %copy.9.counts_ref, bf16[8,64,128,128]{3,2,1,0:T(8,128)(2,1)} %values_ref.1, bf16[256,128,256]{2,1,0:T(8,128)(2,1)} %bitcast.39), custom_call_target="tpu_custom_call" | custom-call | flops 4294967296 | bytes 34603008 | tf_op jit(solution)/shard_map/pallas_call | solution.py:90
  152.4 0.0 copy-done
  152.4 0.8 convolution_multiply_fusion
  153.2 0.4 collective-permute-start.1
  153.6 1.0 collective-permute-done.1
  154.7 5.0 %collective-permute-start.4 = (f32[128,256]{1,0:T(8,128)S(1)}, f32[128,256]{1,0:T(8,128)S(1)}, u32[]{:S(2)}, u32[]{:S(2)}) collective-permute-start(f32[128,256]{1,0:T(8,128)S(1)} %bitcast_add_fusion.1), channel_id=1, source_target_pairs={{0,5},{1,4},{2,7},{3,6},{4,1},{5,0},{6,3},{7,2},{8,13},{9,12},{10,... | collective-permute-start | bytes 393224 | tf_op jit(solution)/shard_map/ppermute | solution.py:40
  159.7 0.0 collective-permute-start.3
  159.7 0.7 collective-permute-start.2
  160.4 2.4 %collective-permute-start = (f32[512,256]{1,0:T(8,128)S(1)}, f32[512,256]{1,0:T(8,128)}, u32[]{:S(2)}, u32[]{:S(2)}) collective-permute-start(f32[512,256]{1,0:T(8,128)S(1)} %select_bitcast_fusion), channel_id=1, source_target_pairs={{0,1},{1,0},{2,3},{3,2},{4,5},{5,4},{6,7},{7,6},{8,9},{9,8},{10,11... | collective-permute-start | bytes 1572872 | tf_op jit(solution)/shard_map/ppermute | solution.py:120
  162.9 2.4 %collective-permute-done.4 = f32[128,256]{1,0:T(8,128)S(1)} collective-permute-done((f32[128,256]{1,0:T(8,128)S(1)}, f32[128,256]{1,0:T(8,128)S(1)}, u32[]{:S(2)}, u32[]{:S(2)}) %collective-permute-start.4) | collective-permute-done | bytes 131104 | tf_op jit(solution)/shard_map/ppermute | solution.py:40
  165.2 0.6 collective-permute-done.3
  165.9 0.8 collective-permute-done.2
  166.7 0.6 gather_fusion
  167.3 0.1 broadcast_select_fusion.2
  167.5 0.1 collective-permute-start.7
  167.6 1.5 collective-permute-start.6
  169.1 1.7 collective-permute-start.5
  170.9 4.3 %collective-permute-done.7 = f32[128,256]{1,0:T(8,128)S(1)} collective-permute-done((f32[128,256]{1,0:T(8,128)S(1)}, f32[128,256]{1,0:T(8,128)S(1)}, u32[]{:S(2)}, u32[]{:S(2)}) %collective-permute-start.7) | collective-permute-done | bytes 131104 | tf_op jit(solution)/shard_map/ppermute | solution.py:40
  175.1 0.0 collective-permute-done.6
  175.2 0.4 collective-permute-done.5
  175.6 0.6 gather_fusion.1
  176.2 0.1 broadcast_select_fusion.1
  176.3 1.2 collective-permute-start.10
  177.5 0.9 collective-permute-start.9
  178.4 1.2 collective-permute-start.8
  179.7 1.7 collective-permute-done.10
  181.4 1.4 collective-permute-done.9
  182.9 0.8 collective-permute-done.8
  183.7 0.6 gather_fusion.2
  184.3 0.1 broadcast_select_fusion
  184.5 3.9 %collective-permute-start.11 = (f32[128,256]{1,0:T(8,128)S(1)}, f32[128,256]{1,0:T(8,128)S(1)}, u32[]{:S(2)}, u32[]{:S(2)}) collective-permute-start(f32[128,256]{1,0:T(8,128)S(1)} %fusion.4), channel_id=1, source_target_pairs={{0,2},{1,3},{2,0},{3,1},{4,6},{5,7},{6,4},{7,5},{8,10},{9,11},{10,... | collective-permute-start | bytes 393224 | tf_op jit(solution)/shard_map/ppermute | solution.py:46
  188.3 0.0 collective-permute-done
  188.4 0.0 copy-done.2
  188.4 2.0 %convolution_convert_fusion = bf16[512,256]{1,0:T(8,128)(2,1)} fusion(bf16[256,256]{1,0:T(8,128)(2,1)S(1)} %copy-done.2, f32[512,256]{1,0:T(8,128)} %collective-permute-done, f32[2,512,256]{2,1,0:T(8,128)S(1)} %bitcast.38, s32[]{:T(128)S(6)} %select_n.46, pred[]{:T(512)S(6)} %and.48), kind=kOutput, calls=%fused_computation.3 | convolution fusion | flops 67633152 | bytes 1441797 | tf_op jit(solution)/shard_map/dot_general | solution.py:122
  190.4 0.0 collective-permute-done.11
  190.4 0.7 maximum_select_fusion
  (19 shorter events, 0.4 us)
Async XLA Ops:
  7.2 145.2 %copy-start = (bf16[1024,256]{1,0:T(8,128)(2,1)S(1)}, bf16[1024,256]{1,0:T(8,128)(2,1)}, u32[]{:S(2)}) copy-start(bf16[1024,256]{1,0:T(8,128)(2,1)} %param.15) | copy-start | bytes 1572868
  7.2 128.6 %all-gather.2.cloned.1.call-start = ((), (), s32[]{:S(2)}) async-start(), calls=%async_computation | async-start | bytes 17039360 | tf_op jit(solution)/shard_map/all_gather | solution.py:108
  135.8 0.7 copy-start.1
  136.5 51.9 %copy-start.2 = (bf16[256,256]{1,0:T(8,128)(2,1)S(1)}, bf16[256,256]{1,0:T(8,128)(2,1)}, u32[]{:S(2)}) copy-start(bf16[256,256]{1,0:T(8,128)(2,1)} %param.16) | copy-start | bytes 393220
  153.2 1.4 collective-permute-start.1
  154.7 10.5 %collective-permute-start.4 = (f32[128,256]{1,0:T(8,128)S(1)}, f32[128,256]{1,0:T(8,128)S(1)}, u32[]{:S(2)}, u32[]{:S(2)}) collective-permute-start(f32[128,256]{1,0:T(8,128)S(1)} %bitcast_add_fusion.1), channel_id=1, source_target_pairs={{0,5},{1,4},{2,7},{3,6},{4,1},{5,0},{6,3},{7,2},{8,13},{9,12},{10,... | collective-permute-start | bytes 393224 | tf_op jit(solution)/shard_map/ppermute | solution.py:40
  159.7 6.1 %collective-permute-start.3 = (f32[128,256]{1,0:T(8,128)S(1)}, f32[128,256]{1,0:T(8,128)S(1)}, u32[]{:S(2)}, u32[]{:S(2)}) collective-permute-start(f32[128,256]{1,0:T(8,128)S(1)} %bitcast_add_fusion.1), channel_id=1, source_target_pairs={{0,1},{1,0},{2,3},{3,2},{4,5},{5,4},{6,7},{7,6},{8,9},{9,8},{10,11... | collective-permute-start | bytes 393224 | tf_op jit(solution)/shard_map/ppermute | solution.py:40
  159.7 7.0 %collective-permute-start.2 = (f32[128,256]{1,0:T(8,128)S(1)}, f32[128,256]{1,0:T(8,128)S(1)}, u32[]{:S(2)}, u32[]{:S(2)}) collective-permute-start(f32[128,256]{1,0:T(8,128)S(1)} %bitcast_add_fusion.1), channel_id=1, source_target_pairs={{0,4},{1,5},{2,6},{3,7},{4,0},{5,1},{6,2},{7,3},{8,12},{9,13},{10,... | collective-permute-start | bytes 393224 | tf_op jit(solution)/shard_map/ppermute | solution.py:40
  160.4 27.9 %collective-permute-start = (f32[512,256]{1,0:T(8,128)S(1)}, f32[512,256]{1,0:T(8,128)}, u32[]{:S(2)}, u32[]{:S(2)}) collective-permute-start(f32[512,256]{1,0:T(8,128)S(1)} %select_bitcast_fusion), channel_id=1, source_target_pairs={{0,1},{1,0},{2,3},{3,2},{4,5},{5,4},{6,7},{7,6},{8,9},{9,8},{10,11... | collective-permute-start | bytes 1572872 | tf_op jit(solution)/shard_map/ppermute | solution.py:120
  167.5 7.7 %collective-permute-start.7 = (f32[128,256]{1,0:T(8,128)S(1)}, f32[128,256]{1,0:T(8,128)S(1)}, u32[]{:S(2)}, u32[]{:S(2)}) collective-permute-start(f32[128,256]{1,0:T(8,128)S(1)} %fusion.11), channel_id=1, source_target_pairs={{0,24},{1,25},{2,26},{3,27},{4,28},{5,29},{6,30},{7,31},{8,16},{9,... | collective-permute-start | bytes 393224 | tf_op jit(solution)/shard_map/ppermute | solution.py:40
  167.6 7.6 %collective-permute-start.6 = (f32[128,256]{1,0:T(8,128)S(1)}, f32[128,256]{1,0:T(8,128)S(1)}, u32[]{:S(2)}, u32[]{:S(2)}) collective-permute-start(f32[128,256]{1,0:T(8,128)S(1)} %fusion.11), channel_id=1, source_target_pairs={{0,16},{1,17},{2,18},{3,19},{4,20},{5,21},{6,22},{7,23},{8,24},{9,... | collective-permute-start | bytes 393224 | tf_op jit(solution)/shard_map/ppermute | solution.py:40
  169.1 6.4 %collective-permute-start.5 = (f32[128,256]{1,0:T(8,128)S(1)}, f32[128,256]{1,0:T(8,128)S(1)}, u32[]{:S(2)}, u32[]{:S(2)}) collective-permute-start(f32[128,256]{1,0:T(8,128)S(1)} %fusion.11), channel_id=1, source_target_pairs={{0,8},{1,9},{2,10},{3,11},{4,12},{5,13},{6,14},{7,15},{8,0},{9,1},... | collective-permute-start | bytes 393224 | tf_op jit(solution)/shard_map/ppermute | solution.py:40
  176.3 5.1 %collective-permute-start.10 = (f32[128,256]{1,0:T(8,128)S(1)}, f32[128,256]{1,0:T(8,128)S(1)}, u32[]{:S(2)}, u32[]{:S(2)}) collective-permute-start(f32[128,256]{1,0:T(8,128)S(1)} %fusion.10), channel_id=1, source_target_pairs={{0,96},{1,97},{2,98},{3,99},{4,100},{5,101},{6,102},{7,103},{8,104... | collective-permute-start | bytes 393224 | tf_op jit(solution)/shard_map/ppermute | solution.py:40
  177.5 5.3 %collective-permute-start.9 = (f32[128,256]{1,0:T(8,128)S(1)}, f32[128,256]{1,0:T(8,128)S(1)}, u32[]{:S(2)}, u32[]{:S(2)}) collective-permute-start(f32[128,256]{1,0:T(8,128)S(1)} %fusion.10), channel_id=1, source_target_pairs={{0,64},{1,65},{2,66},{3,67},{4,68},{5,69},{6,70},{7,71},{8,72},{9,... | collective-permute-start | bytes 393224 | tf_op jit(solution)/shard_map/ppermute | solution.py:40
  178.4 5.3 %collective-permute-start.8 = (f32[128,256]{1,0:T(8,128)S(1)}, f32[128,256]{1,0:T(8,128)S(1)}, u32[]{:S(2)}, u32[]{:S(2)}) collective-permute-start(f32[128,256]{1,0:T(8,128)S(1)} %fusion.10), channel_id=1, source_target_pairs={{0,32},{1,33},{2,34},{3,35},{4,36},{5,37},{6,38},{7,39},{8,40},{9,... | collective-permute-start | bytes 393224 | tf_op jit(solution)/shard_map/ppermute | solution.py:40
  184.5 5.9 %collective-permute-start.11 = (f32[128,256]{1,0:T(8,128)S(1)}, f32[128,256]{1,0:T(8,128)S(1)}, u32[]{:S(2)}, u32[]{:S(2)}) collective-permute-start(f32[128,256]{1,0:T(8,128)S(1)} %fusion.4), channel_id=1, source_target_pairs={{0,2},{1,3},{2,0},{3,1},{4,6},{5,7},{6,4},{7,5},{8,10},{9,11},{10,... | collective-permute-start | bytes 393224 | tf_op jit(solution)/shard_map/ppermute | solution.py:46
Sparse Core Ops, SparseCore 0:
  10.3 125.4 all-gather.1
